TPU v7x, 256 devices: a whole 4x4x8 slice. The times are simulated.
256 devices in a mesh: dp: 2 (over core), expert: 128 (over x, z, y).
Axes of the slice: x: 4, y: 4, z: 8, core: 2. Of those that a mesh axis runs over, the one named last changes fastest.
Arguments:
- states: bfloat16 [3, 32768, 1024], P(None, ('dp', 'expert')), may hold values from -6 to 6
- language: int32 [3, 32768, 1], P(None, ('dp', 'expert')), may hold values from 0 to 127; in each aligned block of 128 rows (0 to 127, 128 to 255, ..., all dimensions but the last counted through in order) at most 2 rows name the same one
- placement: int32 [3, 128], replicated, may hold values from 0 to 127, each once within a row
- swap_flags: int32 [128], replicated, may hold values from 0 to 1, as said below
- up_weight: bfloat16 [128, 1024, 4096], P('expert', None, 'dp'), may hold values from -0.1875 to 0.1875
- down_weight: bfloat16 [128, 4096, 1024], P('expert', 'dp'), may hold values from -0.09375 to 0.09375
Outputs:
- updated: bfloat16 [3, 32768, 1024], P(None, ('dp', 'expert'))
Inputs may be any that keep to these rules, and one draw needn't show every extreme that they name: In the 128 rows of one device at one step (aligned blocks along the rows), no language id occurs more than 2 times, and some id occurs exactly 2 times. `placement`: each step's row is a permutation of the devices of the expert axis. swap_flags[j] equals swap_flags[j + 64] for j under 128/2.
All inputs are finite; a program needn't handle non-finite values.
Results may differ from a plain program's by a relative error of at most 0.0047.
Values may be sent and summed in bfloat16 or wider, within the bound.
No kernel may reach another device: no remote copies, remote signals or barrier semaphores. Data moves between devices by JAX's collectives and lax.ppermute only.
A program may use at most 128 MiB of HBM per device.

v0:
```python
import jax
import jax.numpy as jnp
from jax import lax
from jax.sharding import PartitionSpec as P


def shifted(value, axis, by):
    devices = lax.axis_size(axis)
    return lax.ppermute(value, axis, [(i, (i + by) % devices) for i in range(devices)])


def make_expert(up_matrix, down_matrix):

    def apply_rows(shard_rows):
        hidden = jnp.maximum(
            jnp.dot(shard_rows, up_matrix, preferred_element_type=jnp.float32), 0.0
        ).astype(jnp.bfloat16)
        return jnp.dot(hidden, down_matrix, preferred_element_type=jnp.float32)

    def expert_fn(arrived):
        source_count, slot_count, model_width = arrived.shape
        flat_rows = arrived.reshape(source_count * slot_count, model_width)
        partial_terms = apply_rows(lax.all_gather(flat_rows, "dp", axis=0, tiled=True))
        own_share = lax.psum_scatter(partial_terms, "dp", scatter_dimension=0, tiled=True)
        return own_share.astype(jnp.bfloat16).reshape(source_count, slot_count, model_width)

    return expert_fn


def shards(states, language, placement, swap_flags, up_weight, down_weight):
    step_count, row_count, model_width = states.shape
    experts = lax.axis_size("expert")
    capacity = max(2, 2 * row_count // experts)
    labels = jnp.arange(experts, dtype=jnp.int32)
    up_local = up_weight[0]
    down_local = down_weight[0]
    own_flag = jnp.sum(jnp.where(labels == lax.axis_index("expert"), swap_flags, 0))
    partner_up, partner_down = shifted((up_local, down_local), "expert", experts // 2)
    later_up = jnp.where(own_flag == 1, partner_up, up_local)
    later_down = jnp.where(own_flag == 1, partner_down, down_local)
    slot_labels = jnp.arange(experts * capacity, dtype=jnp.int32)
    outputs = []
    for step_index in range(step_count):
        lang_hot = (language[step_index, :, 0][:, None] == labels[None, :]).astype(jnp.int32)
        target = jnp.sum(lang_hot * placement[step_index][None, :], axis=1)
        dest_hot = (target[:, None] == labels[None, :]).astype(jnp.int32)
        earlier = jnp.cumsum(dest_hot, axis=0) - dest_hot
        position_in = jnp.sum(earlier * dest_hot, axis=1)
        slot_index = target * capacity + position_in
        select = (slot_index[:, None] == slot_labels[None, :]).astype(jnp.bfloat16)
        outgoing = jnp.einsum(
            "rs,rd->sd", select, states[step_index], preferred_element_type=jnp.float32
        )
        outgoing = outgoing.astype(jnp.bfloat16).reshape(experts, capacity, model_width)
        if step_index == 0:
            expert_fn = make_expert(up_local, down_local)
        else:
            expert_fn = make_expert(later_up, later_down)
        served = expert_fn(
            lax.all_to_all(outgoing, "expert", split_axis=0, concat_axis=0, tiled=True)
        )
        returned = lax.all_to_all(served, "expert", split_axis=0, concat_axis=0, tiled=True)
        selected = jnp.dot(
            select,
            returned.reshape(experts * capacity, model_width),
            preferred_element_type=jnp.float32,
        )
        outputs.append((states[step_index].astype(jnp.float32) + selected).astype(jnp.bfloat16))
    return jnp.stack(outputs)


def solution(mesh):
    placed = (
        P(None, ("dp", "expert"), None),
        P(None, ("dp", "expert"), None),
        P(),
        P(),
        P("expert", None, "dp"),
        P("expert", "dp", None),
    )
    return jax.shard_map(
        shards,
        mesh=mesh,
        in_specs=placed,
        out_specs=P(None, ("dp", "expert"), None),
        check_vma=False,
    )
```

profile of v0, /device:TPU:32, one launch (start us, length us, event | category | flops | bytes accessed | tf_op | source)
XLA Modules:
  0.0 393.2 jit_solution(13204717779632014971)
XLA Ops:
  6.5 0.8 slice_bitcast_fusion.5
  7.3 0.8 slice_bitcast_fusion.4
  8.7 1.4 convolution_convert_fusion.2
  10.1 1.0 reshape.60
  11.1 15.0 %all-to-all-start = ((bf16[128,2,1024]{2,1,0:T(2,128)(2,1)}), bf16[128,2,1024]{2,1,0:T(2,128)(2,1)S(1)}, u32[]{:S(2)}, u32[]{:S(2)}) async-start(bf16[128,2,1024]{2,1,0:T(2,128)(2,1)} %reshape.60), calls=%async_computation | async-start | bytes 1048576 | tf_op jit(solution)/shard_map/all_to_all | solution.py:60
  26.8 18.4 %all-to-all-done = bf16[128,2,1024]{2,1,0:T(2,128)(2,1)S(1)} async-done(((bf16[128,2,1024]{2,1,0:T(2,128)(2,1)}), bf16[128,2,1024]{2,1,0:T(2,128)(2,1)S(1)}, u32[]{:S(2)}, u32[]{:S(2)}) %all-to-all-start) | async-done | bytes 524320 | tf_op jit(solution)/shard_map/all_to_all | solution.py:60
  45.2 1.0 reshape.61
  46.3 0.4 convolution_convert_fusion.1
  46.7 1.0 reshape.64
  47.7 7.2 %all-to-all-start.2 = ((bf16[128,2,1024]{2,1,0:T(2,128)(2,1)}), bf16[128,2,1024]{2,1,0:T(2,128)(2,1)S(1)}, u32[]{:S(2)}, u32[]{:S(2)}) async-start(bf16[128,2,1024]{2,1,0:T(2,128)(2,1)} %reshape.64), calls=%async_computation.3 | async-start | bytes 1048576 | tf_op jit(solution)/shard_map/all_to_all | solution.py:60
  55.4 17.4 %all-to-all-done.2 = bf16[128,2,1024]{2,1,0:T(2,128)(2,1)S(1)} async-done(((bf16[128,2,1024]{2,1,0:T(2,128)(2,1)}), bf16[128,2,1024]{2,1,0:T(2,128)(2,1)S(1)}, u32[]{:S(2)}, u32[]{:S(2)}) %all-to-all-start.2) | async-done | bytes 524320 | tf_op jit(solution)/shard_map/all_to_all | solution.py:60
  72.8 1.0 reshape.65
  73.9 0.4 convolution_convert_fusion
  74.3 1.0 reshape.68
  75.3 7.2 %all-to-all-start.4 = ((bf16[128,2,1024]{2,1,0:T(2,128)(2,1)}), bf16[128,2,1024]{2,1,0:T(2,128)(2,1)S(1)}, u32[]{:S(2)}, u32[]{:S(2)}) async-start(bf16[128,2,1024]{2,1,0:T(2,128)(2,1)} %reshape.68), calls=%async_computation.6 | async-start | bytes 1048576 | tf_op jit(solution)/shard_map/all_to_all | solution.py:60
  82.5 3.4 collective-permute-start
  85.9 0.2 collective-permute-start.1
  86.1 13.4 %all-to-all-done.4 = bf16[128,2,1024]{2,1,0:T(2,128)(2,1)S(1)} async-done(((bf16[128,2,1024]{2,1,0:T(2,128)(2,1)}), bf16[128,2,1024]{2,1,0:T(2,128)(2,1)S(1)}, u32[]{:S(2)}, u32[]{:S(2)}) %all-to-all-start.4) | async-done | bytes 524320 | tf_op jit(solution)/shard_map/all_to_all | solution.py:60
  99.5 1.0 reshape.69
  100.6 0.2 reduce-scatter.4.cloned.1.call-start
  100.8 9.7 %fusion.8 = f32[512,1024]{1,0:T(8,128)} fusion(bf16[512,1024]{1,0:T(8,128)(2,1)} %all-gather.4.cloned.1.call-done, bf16[1,2048,1024]{2,1,0:T(8,128)(2,1)} %param.11, bf16[1,1024,2048]{2,1,0:T(8,128)(2,1)} %param.10), kind=kOutput, calls=%fused_computation.19 | convolution fusion | flops 4297064448 | bytes 11534336 | tf_op jit(solution)/shard_map/dot_general | solution.py:18
  110.6 0.7 fusion.24
  111.9 69.6 %collective-permute-done = bf16[1024,2048]{1,0:T(8,128)(2,1)} collective-permute-done((bf16[1024,2048]{1,0:T(8,128)(2,1)}, bf16[1024,2048]{1,0:T(8,128)(2,1)}, u32[]{:S(2)}, u32[]{:S(2)}) %collective-permute-start) | collective-permute-done | bytes 4194336 | tf_op jit(solution)/shard_map/ppermute | solution.py:9
  181.4 87.7 %collective-permute-done.1 = bf16[2048,1024]{1,0:T(8,128)(2,1)} collective-permute-done((bf16[2048,1024]{1,0:T(8,128)(2,1)}, bf16[2048,1024]{1,0:T(8,128)(2,1)}, u32[]{:S(2)}, u32[]{:S(2)}) %collective-permute-start.1) | collective-permute-done | bytes 4194336 | tf_op jit(solution)/shard_map/ppermute | solution.py:9
  269.2 9.6 %fusion.1 = f32[512,1024]{1,0:T(8,128)} fusion(bf16[2048,1024]{1,0:T(8,128)(2,1)} %collective-permute-done.1, pred[]{:T(512)S(6)} %eq.155, bf16[512,1024]{1,0:T(8,128)(2,1)} %all-gather.6.cloned.1.call-done, bf16[1024,2048]{1,0:T(8,128)(2,1)} %collective-permute-done, bf16[1,2048,1024]{2,1,0:T(8,128)(2,1)} %param.11, bf16[1,1024,2048]{2,1,0:T(8,128)(2,1)} %param.10), kind=kOutput, calls=%fused_computation.6 | convolution fusion | flops 4301258752 | bytes 19922944 | tf_op jit(solution)/shard_map/dot_general | solution.py:18
  278.9 4.3 %all-gather.8.cloned.1.call-done = bf16[512,1024]{1,0:T(8,128)(2,1)} async-done(((bf16[256,1024]{1,0:T(8,128)(2,1)}), bf16[512,1024]{1,0:T(8,128)(2,1)}) %all-gather.8.cloned.1.call-update) | async-done | bytes 1048592 | tf_op jit(solution)/shard_map/all_gather | solution.py:23
  283.1 9.6 %fusion = f32[512,1024]{1,0:T(8,128)} fusion(bf16[2048,1024]{1,0:T(8,128)(2,1)} %collective-permute-done.1, pred[]{:T(512)S(6)} %eq.155, bf16[512,1024]{1,0:T(8,128)(2,1)} %all-gather.8.cloned.1.call-done, bf16[1024,2048]{1,0:T(8,128)(2,1)} %collective-permute-done, bf16[1,2048,1024]{2,1,0:T(8,128)(2,1)} %param.11, bf16[1,1024,2048]{2,1,0:T(8,128)(2,1)} %param.10), kind=kOutput, calls=%fused_computation.5 | convolution fusion | flops 4301258752 | bytes 19922944 | tf_op jit(solution)/shard_map/dot_general | solution.py:18
  292.7 9.0 %reduce-scatter.4.cloned.1.call-done = f32[256,1024]{1,0:T(8,128)} async-done(((f32[512,1024]{1,0:T(8,128)}), f32[256,1024]{1,0:T(8,128)}) %reduce-scatter.4.cloned.1.call-update) | async-done | bytes 1048592 | tf_op jit(solution)/shard_map/reduce_scatter | solution.py:24
  301.7 1.3 convert_element_type.64
  303.1 1.0 reshape.62
  304.0 15.4 %all-to-all-start.1 = ((bf16[128,2,1024]{2,1,0:T(2,128)(2,1)}), bf16[128,2,1024]{2,1,0:T(2,128)(2,1)S(1)}, u32[]{:S(2)}, u32[]{:S(2)}) async-start(bf16[128,2,1024]{2,1,0:T(2,128)(2,1)} %reshape.62), calls=%async_computation.2 | async-start | bytes 1048576 | tf_op jit(solution)/shard_map/all_to_all | solution.py:62
  319.5 1.1 reduce-scatter.6.cloned.1.call-done
  320.5 1.3 convert_element_type.70
  321.8 1.0 reshape.66
  322.9 14.5 %all-to-all-done.1 = bf16[128,2,1024]{2,1,0:T(2,128)(2,1)S(1)} async-done(((bf16[128,2,1024]{2,1,0:T(2,128)(2,1)}), bf16[128,2,1024]{2,1,0:T(2,128)(2,1)S(1)}, u32[]{:S(2)}, u32[]{:S(2)}) %all-to-all-start.1) | async-done | bytes 524320 | tf_op jit(solution)/shard_map/all_to_all | solution.py:62
  337.3 7.2 %all-to-all-start.3 = ((bf16[128,2,1024]{2,1,0:T(2,128)(2,1)}), bf16[128,2,1024]{2,1,0:T(2,128)(2,1)S(1)}, u32[]{:S(2)}, u32[]{:S(2)}) async-start(bf16[128,2,1024]{2,1,0:T(2,128)(2,1)} %reshape.66), calls=%async_computation.5 | async-start | bytes 1048576 | tf_op jit(solution)/shard_map/all_to_all | solution.py:62
  344.5 1.3 convert_element_type.76
  345.9 1.0 reshape.70
  346.8 14.7 %all-to-all-done.3 = bf16[128,2,1024]{2,1,0:T(2,128)(2,1)S(1)} async-done(((bf16[128,2,1024]{2,1,0:T(2,128)(2,1)}), bf16[128,2,1024]{2,1,0:T(2,128)(2,1)S(1)}, u32[]{:S(2)}, u32[]{:S(2)}) %all-to-all-start.3) | async-done | bytes 524320 | tf_op jit(solution)/shard_map/all_to_all | solution.py:62
  361.5 7.2 %all-to-all-start.5 = ((bf16[128,2,1024]{2,1,0:T(2,128)(2,1)}), bf16[128,2,1024]{2,1,0:T(2,128)(2,1)S(1)}, u32[]{:S(2)}, u32[]{:S(2)}) async-start(bf16[128,2,1024]{2,1,0:T(2,128)(2,1)} %reshape.70), calls=%async_computation.8 | async-start | bytes 1048576 | tf_op jit(solution)/shard_map/all_to_all | solution.py:62
  368.7 0.2 reshape.63
  368.9 0.3 fusion.7
  369.2 0.2 reshape.67
  369.4 0.3 fusion.6
  369.7 15.2 %all-to-all-done.5 = bf16[128,2,1024]{2,1,0:T(2,128)(2,1)S(1)} async-done(((bf16[128,2,1024]{2,1,0:T(2,128)(2,1)}), bf16[128,2,1024]{2,1,0:T(2,128)(2,1)S(1)}, u32[]{:S(2)}, u32[]{:S(2)}) %all-to-all-start.5) | async-done | bytes 524320 | tf_op jit(solution)/shard_map/all_to_all | solution.py:62
  384.9 0.2 reshape.71
  385.1 0.3 fusion.5
  385.4 1.0 pad_maximum_fusion
  (32 shorter events, 2.0 us)
Async XLA Ops:
  6.5 39.7 %copy-start = (bf16[3,128,1024]{2,1,0:T(8,128)(2,1)S(1)}, bf16[3,128,1024]{2,1,0:T(8,128)(2,1)}, u32[]{:S(2)}) copy-start(bf16[3,128,1024]{2,1,0:T(8,128)(2,1)} %param.6) | copy-start | bytes 2359300
  11.1 34.1 %all-to-all-start = ((bf16[128,2,1024]{2,1,0:T(2,128)(2,1)}), bf16[128,2,1024]{2,1,0:T(2,128)(2,1)S(1)}, u32[]{:S(2)}, u32[]{:S(2)}) async-start(bf16[128,2,1024]{2,1,0:T(2,128)(2,1)} %reshape.60), calls=%async_computation | async-start | bytes 1048576 | tf_op jit(solution)/shard_map/all_to_all | solution.py:60
  26.1 74.7 %all-gather.4.cloned.1.call-start = ((), (), s32[]{:S(2)}) async-start(), calls=%async_computation.9 | async-start | bytes 1572864 | tf_op jit(solution)/shard_map/all_gather | solution.py:23
  47.7 25.1 %all-to-all-start.2 = ((bf16[128,2,1024]{2,1,0:T(2,128)(2,1)}), bf16[128,2,1024]{2,1,0:T(2,128)(2,1)S(1)}, u32[]{:S(2)}, u32[]{:S(2)}) async-start(bf16[128,2,1024]{2,1,0:T(2,128)(2,1)} %reshape.64), calls=%async_computation.3 | async-start | bytes 1048576 | tf_op jit(solution)/shard_map/all_to_all | solution.py:60
  54.9 57.0 %all-gather.6.cloned.1.call-start = ((), (), s32[]{:S(2)}) async-start(), calls=%async_computation.11 | async-start | bytes 1572864 | tf_op jit(solution)/shard_map/all_gather | solution.py:23
  75.3 24.3 %all-to-all-start.4 = ((bf16[128,2,1024]{2,1,0:T(2,128)(2,1)}), bf16[128,2,1024]{2,1,0:T(2,128)(2,1)S(1)}, u32[]{:S(2)}, u32[]{:S(2)}) async-start(bf16[128,2,1024]{2,1,0:T(2,128)(2,1)} %reshape.68), calls=%async_computation.6 | async-start | bytes 1048576 | tf_op jit(solution)/shard_map/all_to_all | solution.py:60
  82.4 200.7 %all-gather.8.cloned.1.call-start = ((), (), s32[]{:S(2)}) async-start(), calls=%async_computation.13 | async-start | bytes 1572864 | tf_op jit(solution)/shard_map/all_gather | solution.py:23
  82.5 99.0 %collective-permute-start = (bf16[1024,2048]{1,0:T(8,128)(2,1)}, bf16[1024,2048]{1,0:T(8,128)(2,1)}, u32[]{:S(2)}, u32[]{:S(2)}) collective-permute-start(bf16[1024,2048]{1,0:T(8,128)(2,1)} %bitcast.62), channel_id=1, source_target_pairs={{0,64},{1,65},{2,66},{3,67},{4,68},{5,69},{6,70},{7,71},{8,72},{9,... | collective-permute-start | bytes 12582920 | tf_op jit(solution)/shard_map/ppermute | solution.py:9
  85.9 183.3 %collective-permute-start.1 = (bf16[2048,1024]{1,0:T(8,128)(2,1)}, bf16[2048,1024]{1,0:T(8,128)(2,1)}, u32[]{:S(2)}, u32[]{:S(2)}) collective-permute-start(bf16[2048,1024]{1,0:T(8,128)(2,1)} %bitcast.61), channel_id=1, source_target_pairs={{0,64},{1,65},{2,66},{3,67},{4,68},{5,69},{6,70},{7,71},{8,72},{9,... | collective-permute-start | bytes 12582920 | tf_op jit(solution)/shard_map/ppermute | solution.py:9
  100.6 10.0 %copy-start.1 = (s32[128]{0:T(128)S(1)}, s32[128]{0:T(128)}, u32[]{:S(2)}) copy-start(s32[128]{0:T(128)} %param.9) | copy-start | bytes 1540
  100.6 201.2 %reduce-scatter.4.cloned.1.call-start = ((), (), s32[]{:S(2)}) async-start(), calls=%async_computation.10 | async-start | bytes 3145728 | tf_op jit(solution)/shard_map/reduce_scatter | solution.py:24
  110.5 210.0 %reduce-scatter.6.cloned.1.call-start = ((), (), s32[]{:S(2)}) async-start(), calls=%async_computation.12 | async-start | bytes 3145728 | tf_op jit(solution)/shard_map/reduce_scatter | solution.py:24
  278.8 65.7 %reduce-scatter.8.cloned.1.call-start = ((), (), s32[]{:S(2)}) async-start(), calls=%async_computation.14 | async-start | bytes 3145728 | tf_op jit(solution)/shard_map/reduce_scatter | solution.py:24
  304.0 33.3 %all-to-all-start.1 = ((bf16[128,2,1024]{2,1,0:T(2,128)(2,1)}), bf16[128,2,1024]{2,1,0:T(2,128)(2,1)S(1)}, u32[]{:S(2)}, u32[]{:S(2)}) async-start(bf16[128,2,1024]{2,1,0:T(2,128)(2,1)} %reshape.62), calls=%async_computation.2 | async-start | bytes 1048576 | tf_op jit(solution)/shard_map/all_to_all | solution.py:62
  337.3 24.2 %all-to-all-start.3 = ((bf16[128,2,1024]{2,1,0:T(2,128)(2,1)}), bf16[128,2,1024]{2,1,0:T(2,128)(2,1)S(1)}, u32[]{:S(2)}, u32[]{:S(2)}) async-start(bf16[128,2,1024]{2,1,0:T(2,128)(2,1)} %reshape.66), calls=%async_computation.5 | async-start | bytes 1048576 | tf_op jit(solution)/shard_map/all_to_all | solution.py:62
  361.5 23.4 %all-to-all-start.5 = ((bf16[128,2,1024]{2,1,0:T(2,128)(2,1)}), bf16[128,2,1024]{2,1,0:T(2,128)(2,1)S(1)}, u32[]{:S(2)}, u32[]{:S(2)}) async-start(bf16[128,2,1024]{2,1,0:T(2,128)(2,1)} %reshape.70), calls=%async_computation.8 | async-start | bytes 1048576 | tf_op jit(solution)/shard_map/all_to_all | solution.py:62
Sparse Core Ops, SparseCore 0:
  46.4 9.1 all-gather.3
  74.0 9.1 all-gather.5
  100.7 182.4 all-gather.7
  285.5 16.2 reduce-scatter.3
  304.2 16.2 reduce-scatter.5
  322.9 16.2 reduce-scatter.7
where the time goes:
time: 394 us; the launch traced here: 393 us
  waiting for transfers between devices  265 us (67%)
  starting transfers between devices  63.2 us (16%)
  matrix products  31.8 us (8%)
  between operations  14.4 us (4%)
  local copies, waits for them, and re-layouts  11.2 us (3%)
  other arithmetic  7.17 us (2%)
    ppermute x2, waiting for transfers between devices, shifted(): lax.ppermute(value, axis, [(i, (i + by) % devices) for i in range(devices)])  157 us
    all_to_all x3, waiting for transfers between devices, shards(): lax.all_to_all(outgoing, 'expert', split_axis=0, concat_axis=0, tiled=True)  49.2 us
    all_to_all x3, waiting for transfers between devices, shards(): lax.all_to_all(served, 'expert', split_axis=0, concat_axis=0, tiled=True)  44.3 us
    all_to_all x3, starting transfers between devices, shards(): lax.all_to_all(served, 'expert', split_axis=0, concat_axis=0, tiled=True)  29.8 us
    all_to_all x3, starting transfers between devices, shards(): lax.all_to_all(outgoing, 'expert', split_axis=0, concat_axis=0, tiled=True)  29.4 us
    dot_general x3, matrix products, apply_rows(): return jnp.dot(hidden, down_matrix, preferred_element_type=jnp.float32)  28.9 us
    reduce_scatter x3, waiting for transfers between devices, expert_fn(): lax.psum_scatter(partial_terms, 'dp', scatter_dimension=0, tiled=True)  10.1 us
  transfers between devices with their start and end apart: 14, of which 11 were waited for; matrix products, arithmetic and copies ran while one was open for 11% of the time, Pallas kernels for 0%

commit v1 on v0

--- a/solution.py
+++ b/solution.py
@@ -2,11 +2,6 @@
 import jax.numpy as jnp
 from jax import lax
 from jax.sharding import PartitionSpec as P
-
-
-def shifted(value, axis, by):
-    devices = lax.axis_size(axis)
-    return lax.ppermute(value, axis, [(i, (i + by) % devices) for i in range(devices)])
 
 
 def make_expert(up_matrix, down_matrix):
@@ -32,17 +27,17 @@
     experts = lax.axis_size("expert")
     capacity = max(2, 2 * row_count // experts)
     labels = jnp.arange(experts, dtype=jnp.int32)
-    up_local = up_weight[0]
-    down_local = down_weight[0]
-    own_flag = jnp.sum(jnp.where(labels == lax.axis_index("expert"), swap_flags, 0))
-    partner_up, partner_down = shifted((up_local, down_local), "expert", experts // 2)
-    later_up = jnp.where(own_flag == 1, partner_up, up_local)
-    later_down = jnp.where(own_flag == 1, partner_down, down_local)
+    resident = jnp.where(swap_flags == 1, (labels + experts // 2) % experts, labels)
+    expert_fn = make_expert(up_weight[0], down_weight[0])
     slot_labels = jnp.arange(experts * capacity, dtype=jnp.int32)
     outputs = []
     for step_index in range(step_count):
+        route = placement[step_index]
+        if step_index >= 1:
+            route_hot = (route[:, None] == labels[None, :]).astype(jnp.int32)
+            route = jnp.sum(route_hot * resident[None, :], axis=1)
         lang_hot = (language[step_index, :, 0][:, None] == labels[None, :]).astype(jnp.int32)
-        target = jnp.sum(lang_hot * placement[step_index][None, :], axis=1)
+        target = jnp.sum(lang_hot * route[None, :], axis=1)
         dest_hot = (target[:, None] == labels[None, :]).astype(jnp.int32)
         earlier = jnp.cumsum(dest_hot, axis=0) - dest_hot
         position_in = jnp.sum(earlier * dest_hot, axis=1)
@@ -52,10 +47,6 @@
             "rs,rd->sd", select, states[step_index], preferred_element_type=jnp.float32
         )
         outgoing = outgoing.astype(jnp.bfloat16).reshape(experts, capacity, model_width)
-        if step_index == 0:
-            expert_fn = make_expert(up_local, down_local)
-        else:
-            expert_fn = make_expert(later_up, later_down)
         served = expert_fn(
             lax.all_to_all(outgoing, "expert", split_axis=0, concat_axis=0, tiled=True)
         )

time: 394 us -> 223 us (0.57)
  waiting for transfers between devices: 265 us -> 85.9 us
  blocking collectives: 0 us -> 24.1 us
  starting transfers between devices: 63.2 us -> 49.3 us
    ppermute x2 -> x0, waiting for transfers between devices: 157 us -> none  [shifted(): lax.ppermute(value, axis, [(i, (i + by) % devices) for i in range(devices)])]
    all_to_all x0 -> x1, blocking collectives: none -> 24.1 us  [shards(): lax.all_to_all(outgoing, 'expert', split_axis=0, concat_axis=0, tiled=True)]
    all_to_all x3 -> x2, waiting for transfers between devices: 49.2 us -> 35.8 us  [shards(): lax.all_to_all(outgoing, 'expert', split_axis=0, concat_axis=0, tiled=True)]
    reduce_scatter x3, waiting for transfers between devices: 10.1 us -> 2.83 us  [expert_fn(): lax.psum_scatter(partial_terms, 'dp', scatter_dimension=0, tiled=True)]
    all_to_all x3 -> x2, starting transfers between devices: 29.4 us -> 22.2 us  [shards(): lax.all_to_all(outgoing, 'expert', split_axis=0, concat_axis=0, tiled=True)]
    all_gather x3, waiting for transfers between devices: 4.3 us -> 0.06 us  [expert_fn(): lax.all_gather(flat_rows, 'dp', axis=0, tiled=True)]
  transfers between devices with their start and end apart: 14 -> 11, of which waited for: 11 -> 6; matrix products, arithmetic and copies ran while one was open for 11% -> 19% of each run, Pallas kernels for 0% -> 0%
where the time goes in v1:
time: 223 us
  waiting for transfers between devices  85.9 us (39%)
  starting transfers between devices  49.3 us (22%)
  matrix products  31.8 us (14%)
  blocking collectives  24.1 us (11%)
  between operations  13.7 us (6%)
  local copies, waits for them, and re-layouts  10.3 us (5%)
  other arithmetic  7.39 us (3%)
    all_to_all x3, waiting for transfers between devices, shards(): lax.all_to_all(served, 'expert', split_axis=0, concat_axis=0, tiled=True)  47.1 us
    all_to_all x2, waiting for transfers between devices, shards(): lax.all_to_all(outgoing, 'expert', split_axis=0, concat_axis=0, tiled=True)  35.8 us
    dot_general x3, matrix products, apply_rows(): return jnp.dot(hidden, down_matrix, preferred_element_type=jnp.float32)  28.8 us
    all_to_all x3, starting transfers between devices, shards(): lax.all_to_all(served, 'expert', split_axis=0, concat_axis=0, tiled=True)  26.7 us
    all_to_all x1, blocking collectives, shards(): lax.all_to_all(outgoing, 'expert', split_axis=0, concat_axis=0, tiled=True)  24.1 us
    all_to_all x2, starting transfers between devices, shards(): lax.all_to_all(outgoing, 'expert', split_axis=0, concat_axis=0, tiled=True)  22.2 us
  transfers between devices with their start and end apart: 11, of which 6 were waited for; matrix products, arithmetic and copies ran while one was open for 19% of the time, Pallas kernels for 0%

profile of v1, /device:TPU:32, one launch (start us, length us, event | category | flops | bytes accessed | tf_op | source)
XLA Modules:
  0.0 222.6 jit_solution(7932140155303321953)
XLA Ops:
  6.5 0.8 slice_bitcast_fusion.5
  7.3 0.8 slice_bitcast_fusion.4
  8.1 0.7 compare_select_fusion.2
  8.8 0.2 select_reduce_fusion.5
  9.0 0.2 select_reduce_fusion.4
  9.3 0.2 reduce_window_sum.24
  9.4 0.2 select_reduce_fusion.3
  9.6 1.4 convolution_convert_fusion.1
  11.0 1.0 reshape.69
  12.0 15.0 %all-to-all-start.2 = ((bf16[128,2,1024]{2,1,0:T(2,128)(2,1)}), bf16[128,2,1024]{2,1,0:T(2,128)(2,1)S(1)}, u32[]{:S(2)}, u32[]{:S(2)}) async-start(bf16[128,2,1024]{2,1,0:T(2,128)(2,1)} %reshape.69), calls=%async_computation.3 | async-start | bytes 1048576 | tf_op jit(solution)/shard_map/all_to_all | solution.py:51
  27.3 0.2 reduce_window_sum.25
  27.5 0.2 select_reduce_fusion
  27.7 18.4 %all-to-all-done.2 = bf16[128,2,1024]{2,1,0:T(2,128)(2,1)S(1)} async-done(((bf16[128,2,1024]{2,1,0:T(2,128)(2,1)}), bf16[128,2,1024]{2,1,0:T(2,128)(2,1)S(1)}, u32[]{:S(2)}, u32[]{:S(2)}) %all-to-all-start.2) | async-done | bytes 524320 | tf_op jit(solution)/shard_map/all_to_all | solution.py:51
  46.1 1.0 reshape.70
  47.1 0.4 convolution_convert_fusion
  47.5 1.0 reshape.73
  48.5 7.2 %all-to-all-start.4 = ((bf16[128,2,1024]{2,1,0:T(2,128)(2,1)}), bf16[128,2,1024]{2,1,0:T(2,128)(2,1)S(1)}, u32[]{:S(2)}, u32[]{:S(2)}) async-start(bf16[128,2,1024]{2,1,0:T(2,128)(2,1)} %reshape.73), calls=%async_computation.6 | async-start | bytes 1048576 | tf_op jit(solution)/shard_map/all_to_all | solution.py:51
  55.9 0.2 reduce_window_sum.20
  56.3 17.4 %all-to-all-done.4 = bf16[128,2,1024]{2,1,0:T(2,128)(2,1)S(1)} async-done(((bf16[128,2,1024]{2,1,0:T(2,128)(2,1)}), bf16[128,2,1024]{2,1,0:T(2,128)(2,1)S(1)}, u32[]{:S(2)}, u32[]{:S(2)}) %all-to-all-start.4) | async-done | bytes 524320 | tf_op jit(solution)/shard_map/all_to_all | solution.py:51
  73.7 1.0 reshape.74
  74.7 0.4 convolution_convert_fusion.2
  75.1 0.2 reshape.65
  75.4 24.1 %all_to_all.30 = bf16[128,2,1024]{2,1,0:T(2,128)(2,1)S(1)} all-to-all(bf16[128,2,1024]{2,1,0:T(2,128)(2,1)S(1)} %reshape.65), channel_id=1, replica_groups=mesh['dp'=2,'expert'=128] {'expert'}, dimensions={0} | all-to-all | bytes 1048576 | tf_op jit(solution)/shard_map/all_to_all | solution.py:51
  99.4 1.0 reshape.66
  100.5 0.2 reduce-scatter.6.cloned.1.call-start
  100.7 9.6 %fusion.2 = f32[512,1024]{1,0:T(8,128)} fusion(bf16[1,2048,1024]{2,1,0:T(8,128)(2,1)} %param.11, bf16[512,1024]{1,0:T(8,128)(2,1)} %all-gather.6.cloned.1.call-done, bf16[1,1024,2048]{2,1,0:T(8,128)(2,1)} %param.10), kind=kOutput, calls=%fused_computation.2 | convolution fusion | flops 4297064448 | bytes 11534336 | tf_op jit(solution)/shard_map/dot_general | solution.py:13
  110.4 9.6 %fusion = f32[512,1024]{1,0:T(8,128)} fusion(bf16[1,2048,1024]{2,1,0:T(8,128)(2,1)} %param.11, bf16[512,1024]{1,0:T(8,128)(2,1)} %all-gather.8.cloned.1.call-done, bf16[1,1024,2048]{2,1,0:T(8,128)(2,1)} %param.10), kind=kOutput, calls=%fused_computation | convolution fusion | flops 4297064448 | bytes 11534336 | tf_op jit(solution)/shard_map/dot_general | solution.py:13
  120.1 9.6 %fusion.4 = f32[512,1024]{1,0:T(8,128)} fusion(bf16[1,2048,1024]{2,1,0:T(8,128)(2,1)} %param.11, bf16[512,1024]{1,0:T(8,128)(2,1)} %all-gather.4.cloned.1.call-done, bf16[1,1024,2048]{2,1,0:T(8,128)(2,1)} %param.10), kind=kOutput, calls=%fused_computation.4 | convolution fusion | flops 4297064448 | bytes 11534336 | tf_op jit(solution)/shard_map/dot_general | solution.py:13
  129.8 1.3 convert_element_type.72
  131.1 1.0 reshape.71
  132.1 12.2 %all-to-all-start.3 = ((bf16[128,2,1024]{2,1,0:T(2,128)(2,1)}), bf16[128,2,1024]{2,1,0:T(2,128)(2,1)S(1)}, u32[]{:S(2)}, u32[]{:S(2)}) async-start(bf16[128,2,1024]{2,1,0:T(2,128)(2,1)} %reshape.71), calls=%async_computation.5 | async-start | bytes 1048576 | tf_op jit(solution)/shard_map/all_to_all | solution.py:53
  144.4 2.8 %reduce-scatter.8.cloned.1.call-done = f32[256,1024]{1,0:T(8,128)} async-done(((f32[512,1024]{1,0:T(8,128)}), f32[256,1024]{1,0:T(8,128)}) %reduce-scatter.8.cloned.1.call-update) | async-done | bytes 1048592 | tf_op jit(solution)/shard_map/reduce_scatter | solution.py:19
  147.1 1.3 convert_element_type.78
  148.4 1.0 reshape.75
  149.4 14.5 %all-to-all-done.3 = bf16[128,2,1024]{2,1,0:T(2,128)(2,1)S(1)} async-done(((bf16[128,2,1024]{2,1,0:T(2,128)(2,1)}), bf16[128,2,1024]{2,1,0:T(2,128)(2,1)S(1)}, u32[]{:S(2)}, u32[]{:S(2)}) %all-to-all-start.3) | async-done | bytes 524320 | tf_op jit(solution)/shard_map/all_to_all | solution.py:53
  163.9 7.2 %all-to-all-start.5 = ((bf16[128,2,1024]{2,1,0:T(2,128)(2,1)}), bf16[128,2,1024]{2,1,0:T(2,128)(2,1)S(1)}, u32[]{:S(2)}, u32[]{:S(2)}) async-start(bf16[128,2,1024]{2,1,0:T(2,128)(2,1)} %reshape.75), calls=%async_computation.8 | async-start | bytes 1048576 | tf_op jit(solution)/shard_map/all_to_all | solution.py:53
  171.2 1.3 convert_element_type.66
  172.5 1.0 reshape.67
  173.5 15.9 %all-to-all-done.5 = bf16[128,2,1024]{2,1,0:T(2,128)(2,1)S(1)} async-done(((bf16[128,2,1024]{2,1,0:T(2,128)(2,1)}), bf16[128,2,1024]{2,1,0:T(2,128)(2,1)S(1)}, u32[]{:S(2)}, u32[]{:S(2)}) %all-to-all-start.5) | async-done | bytes 524320 | tf_op jit(solution)/shard_map/all_to_all | solution.py:53
  189.4 7.2 %all-to-all-start.1 = ((bf16[128,2,1024]{2,1,0:T(2,128)(2,1)}), bf16[128,2,1024]{2,1,0:T(2,128)(2,1)S(1)}, u32[]{:S(2)}, u32[]{:S(2)}) async-start(bf16[128,2,1024]{2,1,0:T(2,128)(2,1)} %reshape.67), calls=%async_computation.2 | async-start | bytes 1048576 | tf_op jit(solution)/shard_map/all_to_all | solution.py:53
  196.6 0.2 reshape.72
  196.8 0.2 reshape.76
  197.0 0.3 fusion.22
  197.3 0.3 fusion.21
  197.5 16.7 %all-to-all-done.1 = bf16[128,2,1024]{2,1,0:T(2,128)(2,1)S(1)} async-done(((bf16[128,2,1024]{2,1,0:T(2,128)(2,1)}), bf16[128,2,1024]{2,1,0:T(2,128)(2,1)S(1)}, u32[]{:S(2)}, u32[]{:S(2)}) %all-to-all-start.1) | async-done | bytes 524320 | tf_op jit(solution)/shard_map/all_to_all | solution.py:53
  214.3 0.2 reshape.68
  214.5 0.3 fusion.23
  214.8 1.0 pad_maximum_fusion
  (26 shorter events, 1.0 us)
Async XLA Ops:
  6.5 40.6 %copy-start = (bf16[3,128,1024]{2,1,0:T(8,128)(2,1)S(1)}, bf16[3,128,1024]{2,1,0:T(8,128)(2,1)}, u32[]{:S(2)}) copy-start(bf16[3,128,1024]{2,1,0:T(8,128)(2,1)} %param.6) | copy-start | bytes 2359300
  12.0 34.1 %all-to-all-start.2 = ((bf16[128,2,1024]{2,1,0:T(2,128)(2,1)}), bf16[128,2,1024]{2,1,0:T(2,128)(2,1)S(1)}, u32[]{:S(2)}, u32[]{:S(2)}) async-start(bf16[128,2,1024]{2,1,0:T(2,128)(2,1)} %reshape.69), calls=%async_computation.3 | async-start | bytes 1048576 | tf_op jit(solution)/shard_map/all_to_all | solution.py:51
  27.0 73.7 %all-gather.6.cloned.1.call-start = ((), (), s32[]{:S(2)}) async-start(), calls=%async_computation.11 | async-start | bytes 1572864 | tf_op jit(solution)/shard_map/all_gather | solution.py:18
  48.5 25.1 %all-to-all-start.4 = ((bf16[128,2,1024]{2,1,0:T(2,128)(2,1)}), bf16[128,2,1024]{2,1,0:T(2,128)(2,1)S(1)}, u32[]{:S(2)}, u32[]{:S(2)}) async-start(bf16[128,2,1024]{2,1,0:T(2,128)(2,1)} %reshape.73), calls=%async_computation.6 | async-start | bytes 1048576 | tf_op jit(solution)/shard_map/all_to_all | solution.py:51
  55.8 54.6 %all-gather.8.cloned.1.call-start = ((), (), s32[]{:S(2)}) async-start(), calls=%async_computation.13 | async-start | bytes 1572864 | tf_op jit(solution)/shard_map/all_gather | solution.py:18
  74.7 45.4 %all-gather.4.cloned.1.call-start = ((), (), s32[]{:S(2)}) async-start(), calls=%async_computation.9 | async-start | bytes 1572864 | tf_op jit(solution)/shard_map/all_gather | solution.py:18
  100.5 29.3 %reduce-scatter.6.cloned.1.call-start = ((), (), s32[]{:S(2)}) async-start(), calls=%async_computation.12 | async-start | bytes 3145728 | tf_op jit(solution)/shard_map/reduce_scatter | solution.py:19
  110.3 36.8 %reduce-scatter.8.cloned.1.call-start = ((), (), s32[]{:S(2)}) async-start(), calls=%async_computation.14 | async-start | bytes 3145728 | tf_op jit(solution)/shard_map/reduce_scatter | solution.py:19
  120.0 51.1 %reduce-scatter.4.cloned.1.call-start = ((), (), s32[]{:S(2)}) async-start(), calls=%async_computation.10 | async-start | bytes 3145728 | tf_op jit(solution)/shard_map/reduce_scatter | solution.py:19
  132.1 31.8 %all-to-all-start.3 = ((bf16[128,2,1024]{2,1,0:T(2,128)(2,1)}), bf16[128,2,1024]{2,1,0:T(2,128)(2,1)S(1)}, u32[]{:S(2)}, u32[]{:S(2)}) async-start(bf16[128,2,1024]{2,1,0:T(2,128)(2,1)} %reshape.71), calls=%async_computation.5 | async-start | bytes 1048576 | tf_op jit(solution)/shard_map/all_to_all | solution.py:53
  163.9 25.5 %all-to-all-start.5 = ((bf16[128,2,1024]{2,1,0:T(2,128)(2,1)}), bf16[128,2,1024]{2,1,0:T(2,128)(2,1)S(1)}, u32[]{:S(2)}, u32[]{:S(2)}) async-start(bf16[128,2,1024]{2,1,0:T(2,128)(2,1)} %reshape.75), calls=%async_computation.8 | async-start | bytes 1048576 | tf_op jit(solution)/shard_map/all_to_all | solution.py:53
  189.4 24.9 %all-to-all-start.1 = ((bf16[128,2,1024]{2,1,0:T(2,128)(2,1)}), bf16[128,2,1024]{2,1,0:T(2,128)(2,1)S(1)}, u32[]{:S(2)}, u32[]{:S(2)}) async-start(bf16[128,2,1024]{2,1,0:T(2,128)(2,1)} %reshape.67), calls=%async_computation.2 | async-start | bytes 1048576 | tf_op jit(solution)/shard_map/all_to_all | solution.py:53
Sparse Core Ops, SparseCore 0:
  47.2 9.1 all-gather.5
  74.8 9.1 all-gather.7
  100.6 9.1 all-gather.3
  112.1 16.2 reduce-scatter.5
  130.9 16.2 reduce-scatter.7
  149.5 16.2 reduce-scatter.3

commit v2 on v1

v2 whole, which is shorter than its diff:
```python
import jax
import jax.numpy as jnp
from jax import lax
from jax.sharding import PartitionSpec as P


def shards(states, language, placement, swap_flags, up_weight, down_weight):
    step_count, row_count, model_width = states.shape
    experts = lax.axis_size("expert")
    capacity = max(2, 2 * row_count // experts)
    labels = jnp.arange(experts, dtype=jnp.int32)
    resident = jnp.where(swap_flags == 1, (labels + experts // 2) % experts, labels)
    slot_labels = jnp.arange(experts * capacity, dtype=jnp.int32)
    selects = []
    outgoing = []
    for step_index in range(step_count):
        route = placement[step_index]
        if step_index >= 1:
            route_hot = (route[:, None] == labels[None, :]).astype(jnp.int32)
            route = jnp.sum(route_hot * resident[None, :], axis=1)
        lang_hot = (language[step_index, :, 0][:, None] == labels[None, :]).astype(jnp.int32)
        target = jnp.sum(lang_hot * route[None, :], axis=1)
        dest_hot = (target[:, None] == labels[None, :]).astype(jnp.int32)
        earlier = jnp.cumsum(dest_hot, axis=0) - dest_hot
        position_in = jnp.sum(earlier * dest_hot, axis=1)
        slot_index = target * capacity + position_in
        select = (slot_index[:, None] == slot_labels[None, :]).astype(jnp.bfloat16)
        selects.append(select)
        sent = jnp.einsum(
            "rs,rd->sd", select, states[step_index], preferred_element_type=jnp.float32
        )
        outgoing.append(sent.astype(jnp.bfloat16).reshape(experts, capacity, model_width))
    outgoing = jnp.concatenate(outgoing, axis=1)
    arrived = lax.all_to_all(outgoing, "expert", split_axis=0, concat_axis=0, tiled=True)
    slot_count = step_count * capacity
    flat_rows = arrived.reshape(experts * slot_count, model_width)
    both_halves = lax.all_gather(flat_rows, "dp", axis=0, tiled=True)
    hidden = jnp.maximum(
        jnp.dot(both_halves, up_weight[0], preferred_element_type=jnp.float32), 0.0
    ).astype(jnp.bfloat16)
    partial_terms = jnp.dot(hidden, down_weight[0], preferred_element_type=jnp.float32)
    own_share = lax.psum_scatter(partial_terms, "dp", scatter_dimension=0, tiled=True)
    served = own_share.astype(jnp.bfloat16).reshape(experts, slot_count, model_width)
    returned = lax.all_to_all(served, "expert", split_axis=0, concat_axis=0, tiled=True)
    outputs = []
    for step_index in range(step_count):
        back = returned[:, step_index * capacity:(step_index + 1) * capacity]
        selected = jnp.dot(
            selects[step_index],
            back.reshape(experts * capacity, model_width),
            preferred_element_type=jnp.float32,
        )
        outputs.append((states[step_index].astype(jnp.float32) + selected).astype(jnp.bfloat16))
    return jnp.stack(outputs)


def solution(mesh):
    placed = (
        P(None, ("dp", "expert"), None),
        P(None, ("dp", "expert"), None),
        P(),
        P(),
        P("expert", None, "dp"),
        P("expert", "dp", None),
    )
    return jax.shard_map(
        shards,
        mesh=mesh,
        in_specs=placed,
        out_specs=P(None, ("dp", "expert"), None),
        check_vma=False,
    )
```

time: 223 us -> 222 us (level)
  blocking collectives: 24.1 us -> 133 us
  waiting for transfers between devices: 85.9 us -> 33.6 us
  starting transfers between devices: 49.3 us -> 0.22 us
  matrix products: 31.8 us -> 24.2 us
  local copies, waits for them, and re-layouts: 10.3 us -> 7.7 us
    all_to_all x5 -> x0, waiting for transfers between devices: 82.9 us -> none  [the longest x3 47.1 us: shards(): lax.all_to_all(served, 'expert', split_axis=0, concat_axis=0, tiled=True)]
    all_to_all x0 -> x1, blocking collectives: none -> 66.3 us  [shards(): lax.all_to_all(served, 'expert', split_axis=0, concat_axis=0, tiled=True)]
    all_to_all x5 -> x0, starting transfers between devices: 48.9 us -> none  [the longest x3 26.7 us: shards(): lax.all_to_all(served, 'expert', split_axis=0, concat_axis=0, tiled=True)]
    all_to_all x1, blocking collectives: 24.1 us -> 67.1 us  [shards(): lax.all_to_all(outgoing, 'expert', split_axis=0, concat_axis=0, tiled=True)]
    reduce_scatter x3 -> x1, waiting for transfers between devices: 2.83 us -> 21.3 us  [shards(): lax.psum_scatter(partial_terms, 'dp', scatter_dimension=0, tiled=True)]
    all_gather x3 -> x1, waiting for transfers between devices: 0.06 us -> 12.3 us  [shards(): both_halves = lax.all_gather(flat_rows, 'dp', axis=0, tiled=True)]
    dot_general x6 -> x4, matrix products: 29.6 us -> 21.1 us  [the longest x1 20.3 us: shards(): jnp.dot(hidden, down_weight[0], preferred_element_type=jnp.float32)]
    reshape x12 -> x8, local copies, waits for them, and re-layouts: 8.78 us -> 5.1 us  [the longest x1 2.48 us: shards(): own_share.astype(jnp.bfloat16).reshape(experts, slot_count, model_width)]
  transfers between devices with their start and end apart: 11 -> 2, of which waited for: 6 -> 2; matrix products, arithmetic and copies ran while one was open for 19% -> 0% of each run, Pallas kernels for 0% -> 0%
where the time goes in v2:
time: 222 us; the launch traced here: 221 us
  blocking collectives  133 us (60%)
  waiting for transfers between devices  33.6 us (15%)
  matrix products  24.2 us (11%)
  between operations  13.6 us (6%)
  other arithmetic  8.69 us (4%)
  local copies, waits for them, and re-layouts  7.7 us (3%)
    all_to_all x1, blocking collectives, shards(): lax.all_to_all(outgoing, 'expert', split_axis=0, concat_axis=0, tiled=True)  67.1 us
    all_to_all x1, blocking collectives, shards(): lax.all_to_all(served, 'expert', split_axis=0, concat_axis=0, tiled=True)  66.3 us
    reduce_scatter x1, waiting for transfers between devices, shards(): lax.psum_scatter(partial_terms, 'dp', scatter_dimension=0, tiled=True)  21.3 us
    dot_general x1, matrix products, shards(): jnp.dot(hidden, down_weight[0], preferred_element_type=jnp.float32)  20.3 us
    all_gather x1, waiting for transfers between devices, shards(): both_halves = lax.all_gather(flat_rows, 'dp', axis=0, tiled=True)  12.3 us
  transfers between devices with their start and end apart: 2, of which 2 were waited for; matrix products, arithmetic and copies ran while one was open for 0% of the time, Pallas kernels for 0%

profile of v2, /device:TPU:32, one launch (start us, length us, event | category | flops | bytes accessed | tf_op | source)
XLA Modules:
  0.0 221.4 jit_solution(11768828404427842151)
XLA Ops:
  6.5 0.0 copy-start
  6.5 0.0 all-gather.2.cloned.1.call-start
  6.5 0.7 compare_select_fusion.2
  7.3 0.7 slice_bitcast_fusion.5
  8.0 0.8 slice_bitcast_fusion.4
  8.8 0.2 select_reduce_fusion.5
  9.0 0.2 select_reduce_fusion.1
  9.2 0.1 fusion.19
  9.3 0.2 reduce_window_sum.25
  9.4 0.2 select_reduce_fusion
  9.6 0.2 select_reduce_fusion.4
  9.8 0.1 fusion.22
  9.9 0.2 reduce_window_sum.24
  10.1 0.2 select_reduce_fusion.3
  10.3 0.1 fusion.25
  10.4 0.2 reduce_window_sum.20
  10.5 0.2 select_reduce_fusion.6
  10.7 1.4 convolution_convert_fusion.2
  12.1 0.2 reshape.53
  12.3 1.4 convolution_convert_fusion.1
  13.6 0.2 reshape.54
  13.9 0.0 copy-done
  13.9 0.4 convolution_convert_fusion
  14.3 0.2 reshape.55
  14.5 1.8 pad_maximum_fusion
  16.3 67.1 %all_to_all.10 = bf16[128,6,1024]{2,1,0:T(8,128)(2,1)S(1)} all-to-all(bf16[128,6,1024]{2,1,0:T(8,128)(2,1)S(1)} %pad_maximum_fusion), channel_id=1, replica_groups=mesh['dp'=2,'expert'=128] {'expert'}, dimensions={0} | all-to-all | bytes 3145728 | tf_op jit(solution)/shard_map/all_to_all | solution.py:34
  83.4 1.4 reshape.56
  84.8 0.0 all-gather.2.cloned.1.call-update
  84.8 0.2 reduce-scatter.2.cloned.1.call-start
  85.1 12.3 %all-gather.2.cloned.1.call-done = bf16[1536,1024]{1,0:T(8,128)(2,1)} async-done(((bf16[768,1024]{1,0:T(8,128)(2,1)}), bf16[1536,1024]{1,0:T(8,128)(2,1)}) %all-gather.2.cloned.1.call-update) | async-done | bytes 3145744 | tf_op jit(solution)/shard_map/all_gather | solution.py:37
  97.4 20.3 %fusion = f32[1536,1024]{1,0:T(8,128)} fusion(bf16[1,2048,1024]{2,1,0:T(8,128)(2,1)} %param.11, bf16[1536,1024]{1,0:T(8,128)(2,1)} %all-gather.2.cloned.1.call-done, bf16[1,1024,2048]{2,1,0:T(8,128)(2,1)} %param.10), kind=kOutput, calls=%fused_computation.1 | convolution fusion | flops 12891193344 | bytes 17825792 | tf_op jit(solution)/shard_map/dot_general | solution.py:41
  117.7 0.0 reduce-scatter.2.cloned.1.call-update
  117.7 21.3 %reduce-scatter.2.cloned.1.call-done = f32[768,1024]{1,0:T(8,128)} async-done(((f32[1536,1024]{1,0:T(8,128)}), f32[768,1024]{1,0:T(8,128)}) %reduce-scatter.2.cloned.1.call-update) | async-done | bytes 3145744 | tf_op jit(solution)/shard_map/reduce_scatter | solution.py:42
  138.9 3.3 %convert_element_type.58 = bf16[768,1024]{1,0:T(8,128)(2,1)} convert(f32[768,1024]{1,0:T(8,128)} %reduce-scatter.2.cloned.1.call-done) | non-fusion elementwise | flops 786432 | bytes 4718592 | tf_op jit(solution)/shard_map/convert_element_type | solution.py:43
  142.2 2.5 %reshape.57 = bf16[128,6,1024]{2,1,0:T(8,128)(2,1)S(1)} reshape(bf16[768,1024]{1,0:T(8,128)(2,1)} %convert_element_type.58) | data formatting | bytes 3145728 | tf_op jit(solution)/shard_map/reshape | solution.py:43
  144.7 66.3 %all_to_all.11 = bf16[128,6,1024]{2,1,0:T(8,128)(2,1)S(1)} all-to-all(bf16[128,6,1024]{2,1,0:T(8,128)(2,1)S(1)} %reshape.57), channel_id=1, replica_groups=mesh['dp'=2,'expert'=128] {'expert'}, dimensions={0} | all-to-all | bytes 3145728 | tf_op jit(solution)/shard_map/all_to_all | solution.py:44
  211.0 1.1 fusion.28
  212.1 0.2 reshape.58
  212.3 0.3 fusion.10
  212.6 0.2 reshape.60
  212.8 0.3 fusion.8
  213.1 0.2 reshape.59
  213.3 0.3 fusion.9
  213.6 1.0 pad_maximum_fusion.1
  (3 shorter events, 0.0 us)
Async XLA Ops:
  6.5 7.3 %copy-start = (bf16[3,128,1024]{2,1,0:T(8,128)(2,1)S(1)}, bf16[3,128,1024]{2,1,0:T(8,128)(2,1)}, u32[]{:S(2)}) copy-start(bf16[3,128,1024]{2,1,0:T(8,128)(2,1)} %param.6) | copy-start | bytes 2359300
  6.5 90.8 %all-gather.2.cloned.1.call-start = ((), (), s32[]{:S(2)}) async-start(), calls=%async_computation.3 | async-start | bytes 4718592 | tf_op jit(solution)/shard_map/all_gather | solution.py:37
  84.8 54.1 %reduce-scatter.2.cloned.1.call-start = ((), (), s32[]{:S(2)}) async-start(), calls=%async_computation.4 | async-start | bytes 9437184 | tf_op jit(solution)/shard_map/reduce_scatter | solution.py:42
Sparse Core Ops, SparseCore 0:
  85.0 12.3 all-gather.1
  117.8 21.1 reduce-scatter.1

commit v3 on v2

--- a/solution.py
+++ b/solution.py
@@ -10,6 +10,14 @@
     capacity = max(2, 2 * row_count // experts)
     labels = jnp.arange(experts, dtype=jnp.int32)
     resident = jnp.where(swap_flags == 1, (labels + experts // 2) % experts, labels)
+    pair = [(0, 1), (1, 0)]
+    other_up = lax.ppermute(up_weight[0], "dp", pair)
+    other_down = lax.ppermute(down_weight[0], "dp", pair)
+    first = lax.axis_index("dp") == 0
+    up_full = jnp.where(first, jnp.concatenate([up_weight[0], other_up], axis=1),
+                        jnp.concatenate([other_up, up_weight[0]], axis=1))
+    down_full = jnp.where(first, jnp.concatenate([down_weight[0], other_down], axis=0),
+                          jnp.concatenate([other_down, down_weight[0]], axis=0))
     slot_labels = jnp.arange(experts * capacity, dtype=jnp.int32)
     selects = []
     outgoing = []
@@ -34,13 +42,11 @@
     arrived = lax.all_to_all(outgoing, "expert", split_axis=0, concat_axis=0, tiled=True)
     slot_count = step_count * capacity
     flat_rows = arrived.reshape(experts * slot_count, model_width)
-    both_halves = lax.all_gather(flat_rows, "dp", axis=0, tiled=True)
     hidden = jnp.maximum(
-        jnp.dot(both_halves, up_weight[0], preferred_element_type=jnp.float32), 0.0
+        jnp.dot(flat_rows, up_full, preferred_element_type=jnp.float32), 0.0
     ).astype(jnp.bfloat16)
-    partial_terms = jnp.dot(hidden, down_weight[0], preferred_element_type=jnp.float32)
-    own_share = lax.psum_scatter(partial_terms, "dp", scatter_dimension=0, tiled=True)
-    served = own_share.astype(jnp.bfloat16).reshape(experts, slot_count, model_width)
+    update = jnp.dot(hidden, down_full, preferred_element_type=jnp.float32)
+    served = update.astype(jnp.bfloat16).reshape(experts, slot_count, model_width)
     returned = lax.all_to_all(served, "expert", split_axis=0, concat_axis=0, tiled=True)
     outputs = []
     for step_index in range(step_count):

time: 222 us -> 168 us (0.76)
  blocking collectives: 133 us -> 59.3 us
  waiting for transfers between devices: 33.6 us -> 52.5 us
  starting transfers between devices: 0.22 us -> 15.5 us
  between operations: 13.6 us -> 0.2 us
    all_to_all x1 -> x0, blocking collectives: 67.1 us -> none  [shards(): lax.all_to_all(outgoing, 'expert', split_axis=0, concat_axis=0, tiled=True)]
    all_to_all x0 -> x1, waiting for transfers between devices: none -> 52.5 us  [shards(): lax.all_to_all(outgoing, 'expert', split_axis=0, concat_axis=0, tiled=True)]
    reduce_scatter x1 -> x0, waiting for transfers between devices: 21.3 us -> none  [shards(): lax.psum_scatter(partial_terms, 'dp', scatter_dimension=0, tiled=True)]
    all_to_all x0 -> x1, starting transfers between devices: none -> 15 us  [shards(): lax.all_to_all(outgoing, 'expert', split_axis=0, concat_axis=0, tiled=True)]
    all_gather x1 -> x0, waiting for transfers between devices: 12.3 us -> none  [shards(): both_halves = lax.all_gather(flat_rows, 'dp', axis=0, tiled=True)]
    all_to_all x1, blocking collectives: 66.3 us -> 59.3 us  [shards(): lax.all_to_all(served, 'expert', split_axis=0, concat_axis=0, tiled=True)]
    convert_element_type x1 -> x0, other arithmetic: 3.29 us -> none  [shards(): own_share.astype(jnp.bfloat16).reshape(experts, slot_count, model_width)]
  transfers between devices with their start and end apart: 2 -> 3, of which waited for: 2 -> 1; matrix products, arithmetic and copies ran while one was open for 0% -> 7% of each run, Pallas kernels for 0% -> 0%
where the time goes in v3:
time: 168 us; the launch traced here: 167 us
  blocking collectives  59.3 us (35%)
  waiting for transfers between devices  52.5 us (31%)
  matrix products  25.4 us (15%)
  starting transfers between devices  15.5 us (9%)
  local copies, waits for them, and re-layouts  7.75 us (5%)
  other arithmetic  6.61 us (4%)
    all_to_all x1, blocking collectives, shards(): lax.all_to_all(served, 'expert', split_axis=0, concat_axis=0, tiled=True)  59.3 us
    all_to_all x1, waiting for transfers between devices, shards(): lax.all_to_all(outgoing, 'expert', split_axis=0, concat_axis=0, tiled=True)  52.5 us
    dot_general x1, matrix products, shards(): update = jnp.dot(hidden, down_full, preferred_element_type=jnp.float32)  21.5 us
    all_to_all x1, starting transfers between devices, shards(): lax.all_to_all(outgoing, 'expert', split_axis=0, concat_axis=0, tiled=True)  15 us
  transfers between devices with their start and end apart: 3, of which 1 were waited for; matrix products, arithmetic and copies ran while one was open for 7% of the time, Pallas kernels for 0%

profile of v3, /device:TPU:32, one launch (start us, length us, event | category | flops | bytes accessed | tf_op | source)
XLA Modules:
  0.0 167.3 jit_solution(11135784460095562659)
XLA Ops:
  0.0 0.0 copy-start
  0.0 0.0 collective-permute-start
  0.0 0.5 collective-permute-start.1
  0.5 0.7 compare_select_fusion.2
  1.2 0.7 slice_bitcast_fusion.5
  1.9 0.8 slice_bitcast_fusion.4
  2.7 0.2 select_reduce_fusion.5
  2.9 0.2 select_reduce_fusion.1
  3.1 0.1 fusion.29
  3.2 0.2 select_reduce_fusion.4
  3.3 0.1 fusion.32
  3.4 0.2 reduce_window_sum.24
  3.6 0.2 select_reduce_fusion.3
  3.8 0.1 fusion.35
  3.9 0.2 reduce_window_sum.20
  4.1 0.2 select_reduce_fusion.6
  4.3 1.4 convolution_convert_fusion.2
  5.6 0.2 reduce_window_sum.25
  5.8 0.2 reshape.53
  6.0 1.4 convolution_convert_fusion.1
  7.4 0.2 reshape.54
  7.6 0.2 select_reduce_fusion
  7.8 0.0 copy-done
  7.8 0.4 convolution_convert_fusion
  8.2 0.2 reshape.55
  8.4 3.1 %pad_maximum_fusion = bf16[128,6,1024]{2,1,0:T(8,128)(2,1)} fusion(bf16[128,2,1024]{2,1,0:T(2,128)(2,1)S(1)} %reshape.55, bf16[128,2,1024]{2,1,0:T(2,128)(2,1)S(1)} %reshape.54, bf16[128,2,1024]{2,1,0:T(2,128)(2,1)S(1)} %reshape.53), kind=kLoop, calls=%fused_computation.17 | loop fusion | flops 4718592 | bytes 3145728 | tf_op jit(solution)/shard_map/concatenate | solution.py:41
  11.5 15.0 %all-to-all-start = ((bf16[128,6,1024]{2,1,0:T(8,128)(2,1)}), bf16[128,6,1024]{2,1,0:T(8,128)(2,1)S(1)}, u32[]{:S(2)}, u32[]{:S(2)}) async-start(bf16[128,6,1024]{2,1,0:T(8,128)(2,1)} %pad_maximum_fusion), calls=%async_computation | async-start | bytes 4194304 | tf_op jit(solution)/shard_map/all_to_all | solution.py:42
  26.5 52.5 %all-to-all-done = bf16[128,6,1024]{2,1,0:T(8,128)(2,1)S(1)} async-done(((bf16[128,6,1024]{2,1,0:T(8,128)(2,1)}), bf16[128,6,1024]{2,1,0:T(8,128)(2,1)S(1)}, u32[]{:S(2)}, u32[]{:S(2)}) %all-to-all-start) | async-done | bytes 1572896 | tf_op jit(solution)/shard_map/all_to_all | solution.py:42
  79.0 1.5 reshape.56
  80.5 0.0 collective-permute-done
  80.5 0.0 collective-permute-done.1
  80.5 21.5 %fusion.14 = bf16[768,1024]{1,0:T(8,128)(2,1)} fusion(bf16[2048,1024]{1,0:T(8,128)(2,1)} %collective-permute-done.1, bf16[2048,1024]{1,0:T(8,128)(2,1)} %bitcast.37, pred[]{:T(512)S(6)} %eq.204, bf16[768,1024]{1,0:T(8,128)(2,1)} %reshape.56, bf16[1024,2048]{1,0:T(8,128)(2,1)} %collective-permute-done, bf16[1024,2048]{1,0:T(8,128)(2,1)} %bitcast.39), kind=kOutput, calls=%fused_computation.18 | convolution fusion | flops 12967477248 | bytes 19922944 | tf_op jit(solution)/shard_map/dot_general | solution.py:48
  102.0 2.5 %reshape.57 = bf16[128,6,1024]{2,1,0:T(8,128)(2,1)S(1)} reshape(bf16[768,1024]{1,0:T(8,128)(2,1)} %fusion.14) | data formatting | bytes 3145728 | tf_op jit(solution)/shard_map/reshape | solution.py:49
  104.5 59.3 %all_to_all.10 = bf16[128,6,1024]{2,1,0:T(8,128)(2,1)S(1)} all-to-all(bf16[128,6,1024]{2,1,0:T(8,128)(2,1)S(1)} %reshape.57), channel_id=1, replica_groups=mesh['dp'=2,'expert'=128] {'expert'}, dimensions={0} | all-to-all | bytes 3145728 | tf_op jit(solution)/shard_map/all_to_all | solution.py:50
  163.8 1.1 fusion.40
  164.9 0.2 reshape.58
  165.1 0.3 fusion.20
  165.3 0.2 reshape.60
  165.5 0.3 fusion.18
  165.8 0.2 reshape.59
  166.0 0.3 fusion.19
  166.3 1.0 pad_maximum_fusion.1
  (3 shorter events, 0.0 us)
Async XLA Ops:
  0.0 7.8 %copy-start = (bf16[3,128,1024]{2,1,0:T(8,128)(2,1)S(1)}, bf16[3,128,1024]{2,1,0:T(8,128)(2,1)}, u32[]{:S(2)}) copy-start(bf16[3,128,1024]{2,1,0:T(8,128)(2,1)} %param.6) | copy-start | bytes 2359300
  0.0 80.5 %collective-permute-start = (bf16[1024,2048]{1,0:T(8,128)(2,1)}, bf16[1024,2048]{1,0:T(8,128)(2,1)}, u32[]{:S(2)}, u32[]{:S(2)}) collective-permute-start(bf16[1024,2048]{1,0:T(8,128)(2,1)} %bitcast.38), channel_id=1, source_target_pairs={{0,128},{128,0},{1,129},{129,1},{2,130},{130,2},{3,131},{131,3},{4... | collective-permute-start | bytes 12582920 | tf_op jit(solution)/shard_map/ppermute | solution.py:14
  0.0 80.5 %collective-permute-start.1 = (bf16[2048,1024]{1,0:T(8,128)(2,1)}, bf16[2048,1024]{1,0:T(8,128)(2,1)}, u32[]{:S(2)}, u32[]{:S(2)}) collective-permute-start(bf16[2048,1024]{1,0:T(8,128)(2,1)} %bitcast.36), channel_id=1, source_target_pairs={{0,128},{128,0},{1,129},{129,1},{2,130},{130,2},{3,131},{131,3},{4... | collective-permute-start | bytes 12582920 | tf_op jit(solution)/shard_map/ppermute | solution.py:15
  11.5 67.6 %all-to-all-start = ((bf16[128,6,1024]{2,1,0:T(8,128)(2,1)}), bf16[128,6,1024]{2,1,0:T(8,128)(2,1)S(1)}, u32[]{:S(2)}, u32[]{:S(2)}) async-start(bf16[128,6,1024]{2,1,0:T(8,128)(2,1)} %pad_maximum_fusion), calls=%async_computation | async-start | bytes 4194304 | tf_op jit(solution)/shard_map/all_to_all | solution.py:42

commit v4 on v3

v4 whole, which is shorter than its diff:
```python
import jax
import jax.numpy as jnp
from jax import lax
from jax.sharding import PartitionSpec as P


def shards(states, language, placement, swap_flags, up_weight, down_weight):
    step_count, row_count, model_width = states.shape
    experts = lax.axis_size("expert")
    capacity = max(2, 2 * row_count // experts)
    labels = jnp.arange(experts, dtype=jnp.int32)
    pair = [(0, 1), (1, 0)]
    other_up = lax.ppermute(up_weight[0], "dp", pair)
    other_down = lax.ppermute(down_weight[0], "dp", pair)
    first = lax.axis_index("dp") == 0
    up_full = jnp.where(first, jnp.concatenate([up_weight[0], other_up], axis=1),
                        jnp.concatenate([other_up, up_weight[0]], axis=1))
    down_full = jnp.where(first, jnp.concatenate([down_weight[0], other_down], axis=0),
                          jnp.concatenate([other_down, down_weight[0]], axis=0))
    resident = jnp.where(swap_flags == 1, (labels + experts // 2) % experts, labels)
    slots_per = step_count * capacity
    slot_ids = []
    for step_index in range(step_count):
        route = placement[step_index]
        if step_index >= 1:
            route_hot = (route[:, None] == labels[None, :]).astype(jnp.int32)
            route = jnp.sum(route_hot * resident[None, :], axis=1)
        lang_hot = (language[step_index, :, 0][:, None] == labels[None, :]).astype(jnp.int32)
        target = jnp.sum(lang_hot * route[None, :], axis=1)
        dest_hot = (target[:, None] == labels[None, :]).astype(jnp.int32)
        earlier = jnp.cumsum(dest_hot, axis=0) - dest_hot
        position_in = jnp.sum(earlier * dest_hot, axis=1)
        slot_ids.append(target * slots_per + step_index * capacity + position_in)
    slot_id = jnp.concatenate(slot_ids)
    slot_labels = jnp.arange(experts * slots_per, dtype=jnp.int32)
    select = (slot_id[:, None] == slot_labels[None, :]).astype(jnp.bfloat16)
    rows = states.reshape(step_count * row_count, model_width)
    outgoing = jnp.einsum("rs,rd->sd", select, rows, preferred_element_type=jnp.float32)
    lanes = 128 if model_width % 128 == 0 else model_width
    packed = (experts, slots_per * model_width // lanes, lanes)
    outgoing = outgoing.astype(jnp.bfloat16).reshape(packed)
    arrived = lax.all_to_all(outgoing, "expert", split_axis=0, concat_axis=0, tiled=True)
    flat_rows = arrived.reshape(experts * slots_per, model_width)
    hidden = jnp.maximum(
        jnp.dot(flat_rows, up_full, preferred_element_type=jnp.float32), 0.0
    ).astype(jnp.bfloat16)
    update = jnp.dot(hidden, down_full, preferred_element_type=jnp.float32)
    served = update.astype(jnp.bfloat16).reshape(packed)
    returned = lax.all_to_all(served, "expert", split_axis=0, concat_axis=0, tiled=True)
    selected = jnp.dot(
        select,
        returned.reshape(experts * slots_per, model_width),
        preferred_element_type=jnp.float32,
    )
    updated = (rows.astype(jnp.float32) + selected).astype(jnp.bfloat16)
    return updated.reshape(step_count, row_count, model_width)


def solution(mesh):
    placed = (
        P(None, ("dp", "expert"), None),
        P(None, ("dp", "expert"), None),
        P(),
        P(),
        P("expert", None, "dp"),
        P("expert", "dp", None),
    )
    return jax.shard_map(
        shards,
        mesh=mesh,
        in_specs=placed,
        out_specs=P(None, ("dp", "expert"), None),
        check_vma=False,
    )
```

time: 168 us -> 142 us (0.85)
  blocking collectives: 59.3 us -> 47.7 us
  waiting for transfers between devices: 52.5 us -> 41.5 us
  other arithmetic: 6.61 us -> 2.57 us
    all_to_all x1, blocking collectives: 59.3 us -> 47.7 us  [shards(): lax.all_to_all(served, 'expert', split_axis=0, concat_axis=0, tiled=True)]
    all_to_all x1, waiting for transfers between devices: 52.5 us -> 41.5 us  [shards(): lax.all_to_all(outgoing, 'expert', split_axis=0, concat_axis=0, tiled=True)]
    concatenate x1, other arithmetic: 3.08 us -> 0.01 us  [shards(): slot_id = jnp.concatenate(slot_ids)]
    dot_general x6 -> x2, matrix products: 3.9 us -> 5.09 us  [the longest x1 2.86 us: shards(): jnp.dot(select, returned.reshape(experts * slots_per, model_width), prefe...]
    reshape x8 -> x4, local copies, waits for them, and re-layouts: 5.16 us -> 6.07 us  [the longest x1 2.55 us: shards(): served = update.astype(jnp.bfloat16).reshape(packed)]
  transfers between devices with their start and end apart: 3 -> 3, of which waited for: 1 -> 1; matrix products, arithmetic and copies ran while one was open for 7% -> 6% of each run, Pallas kernels for 0% -> 0%
where the time goes in v4:
time: 142 us; the launch traced here: 141 us
  blocking collectives  47.7 us (34%)
  waiting for transfers between devices  41.5 us (29%)
  matrix products  26.2 us (18%)
  starting transfers between devices  15.5 us (11%)
  local copies, waits for them, and re-layouts  7.56 us (5%)
  other arithmetic  2.57 us (2%)
    all_to_all x1, blocking collectives, shards(): lax.all_to_all(served, 'expert', split_axis=0, concat_axis=0, tiled=True)  47.7 us
    all_to_all x1, waiting for transfers between devices, shards(): lax.all_to_all(outgoing, 'expert', split_axis=0, concat_axis=0, tiled=True)  41.5 us
    dot_general x1, matrix products, shards(): update = jnp.dot(hidden, down_full, preferred_element_type=jnp.float32)  21.1 us
    all_to_all x1, starting transfers between devices, shards(): lax.all_to_all(outgoing, 'expert', split_axis=0, concat_axis=0, tiled=True)  15 us
    dot_general x1, matrix products, shards(): jnp.dot(select, returned.reshape(experts * slots_per, model_width), prefe...  2.86 us
  transfers between devices with their start and end apart: 3, of which 1 were waited for; matrix products, arithmetic and copies ran while one was open for 6% of the time, Pallas kernels for 0%

profile of v4, /device:TPU:32, one launch (start us, length us, event | category | flops | bytes accessed | tf_op | source)
XLA Modules:
  0.0 141.2 jit_solution(6324283072463184396)
XLA Ops:
  0.0 0.0 collective-permute-start
  0.0 0.5 collective-permute-start.1
  0.5 0.7 compare_select_fusion.2
  1.2 0.7 slice_bitcast_fusion.5
  1.9 0.8 slice_bitcast_fusion.4
  2.7 0.2 select_reduce_fusion.5
  2.9 0.2 select_reduce_fusion.1
  3.1 0.1 fusion.17
  3.2 0.2 reduce_window_sum.25
  3.3 0.2 select_reduce_fusion
  3.5 0.2 select_reduce_fusion.4
  3.7 0.1 fusion.18
  3.8 0.2 reduce_window_sum.24
  4.0 0.2 select_reduce_fusion.3
  4.1 0.1 fusion.19
  4.2 0.2 reduce_window_sum.20
  4.4 0.2 select_reduce_fusion.6
  4.6 2.2 %convolution_convert_fusion = bf16[768,1024]{1,0:T(8,128)(2,1)S(1)} fusion(bf16[384,1024]{1,0:T(8,128)(2,1)} %bitcast.23, s32[384]{0:T(512)S(1)} %pad_add_fusion), kind=kOutput, calls=%fused_computation.18 | convolution fusion | flops 605061120 | bytes 2360832 | tf_op jit(solution)/shard_map/rs,rd->sd/dot_general | solution.py:38
  6.9 2.1 %reshape.31 = bf16[128,48,128]{2,1,0:T(8,128)(2,1)} reshape(bf16[768,1024]{1,0:T(8,128)(2,1)S(1)} %convolution_convert_fusion) | data formatting | bytes 3145728 | tf_op jit(solution)/shard_map/reshape | solution.py:41
  9.0 15.0 %all-to-all-start = ((bf16[128,48,128]{2,1,0:T(8,128)(2,1)}), bf16[128,48,128]{2,1,0:T(8,128)(2,1)S(1)}, u32[]{:S(2)}, u32[]{:S(2)}) async-start(bf16[128,48,128]{2,1,0:T(8,128)(2,1)} %reshape.31), calls=%async_computation | async-start | bytes 3145728 | tf_op jit(solution)/shard_map/all_to_all | solution.py:42
  24.0 41.5 %all-to-all-done = bf16[128,48,128]{2,1,0:T(8,128)(2,1)S(1)} async-done(((bf16[128,48,128]{2,1,0:T(8,128)(2,1)}), bf16[128,48,128]{2,1,0:T(8,128)(2,1)S(1)}, u32[]{:S(2)}, u32[]{:S(2)}) %all-to-all-start) | async-done | bytes 1572896 | tf_op jit(solution)/shard_map/all_to_all | solution.py:42
  65.5 0.7 reshape.32
  66.3 0.0 collective-permute-done
  66.3 0.0 collective-permute-done.1
  66.3 21.1 %fusion.14 = bf16[768,1024]{1,0:T(8,128)(2,1)} fusion(bf16[2048,1024]{1,0:T(8,128)(2,1)} %collective-permute-done.1, bf16[2048,1024]{1,0:T(8,128)(2,1)} %bitcast.20, pred[]{:T(512)S(6)} %eq.172, bf16[768,1024]{1,0:T(8,128)(2,1)S(1)} %reshape.32, bf16[1024,2048]{1,0:T(8,128)(2,1)} %collective-permute-done, bf16[1024,2048]{1,0:T(8,128)(2,1)} %bitcast.22), kind=kOutput, calls=%fused_computation.17 | convolution fusion | flops 12967477248 | bytes 19922944 | tf_op jit(solution)/shard_map/dot_general | solution.py:47
  87.4 2.5 %reshape.33 = bf16[128,48,128]{2,1,0:T(8,128)(2,1)S(1)} reshape(bf16[768,1024]{1,0:T(8,128)(2,1)} %fusion.14) | data formatting | bytes 3145728 | tf_op jit(solution)/shard_map/reshape | solution.py:48
  90.0 47.7 %all_to_all.10 = bf16[128,48,128]{2,1,0:T(8,128)(2,1)S(1)} all-to-all(bf16[128,48,128]{2,1,0:T(8,128)(2,1)S(1)} %reshape.33), channel_id=1, replica_groups=mesh['dp'=2,'expert'=128] {'expert'}, dimensions={0} | all-to-all | bytes 3145728 | tf_op jit(solution)/shard_map/all_to_all | solution.py:49
  137.6 0.7 reshape.34
  138.4 2.9 %add_convert_fusion = bf16[384,1024]{1,0:T(8,128)(2,1)} fusion(bf16[384,1024]{1,0:T(8,128)(2,1)} %bitcast.24, bf16[768,1024]{1,0:T(8,128)(2,1)S(1)} %reshape.34, s32[384]{0:T(512)S(1)} %pad_add_fusion), kind=kOutput, calls=%fused_computation.19 | convolution fusion | flops 605454336 | bytes 3147264 | tf_op jit(solution)/shard_map/dot_general | solution.py:50
  (4 shorter events, 0.0 us)
Async XLA Ops:
  0.0 66.3 %collective-permute-start = (bf16[1024,2048]{1,0:T(8,128)(2,1)}, bf16[1024,2048]{1,0:T(8,128)(2,1)}, u32[]{:S(2)}, u32[]{:S(2)}) collective-permute-start(bf16[1024,2048]{1,0:T(8,128)(2,1)} %bitcast.21), channel_id=1, source_target_pairs={{0,128},{128,0},{1,129},{129,1},{2,130},{130,2},{3,131},{131,3},{4... | collective-permute-start | bytes 12582920 | tf_op jit(solution)/shard_map/ppermute | solution.py:13
  0.0 66.3 %collective-permute-start.1 = (bf16[2048,1024]{1,0:T(8,128)(2,1)}, bf16[2048,1024]{1,0:T(8,128)(2,1)}, u32[]{:S(2)}, u32[]{:S(2)}) collective-permute-start(bf16[2048,1024]{1,0:T(8,128)(2,1)} %bitcast.19), channel_id=1, source_target_pairs={{0,128},{128,0},{1,129},{129,1},{2,130},{130,2},{3,131},{131,3},{4... | collective-permute-start | bytes 12582920 | tf_op jit(solution)/shard_map/ppermute | solution.py:14
  9.0 56.5 %all-to-all-start = ((bf16[128,48,128]{2,1,0:T(8,128)(2,1)}), bf16[128,48,128]{2,1,0:T(8,128)(2,1)S(1)}, u32[]{:S(2)}, u32[]{:S(2)}) async-start(bf16[128,48,128]{2,1,0:T(8,128)(2,1)} %reshape.31), calls=%async_computation | async-start | bytes 3145728 | tf_op jit(solution)/shard_map/all_to_all | solution.py:42

commit v5 on v4

--- a/solution.py
+++ b/solution.py
@@ -19,19 +19,16 @@
                           jnp.concatenate([other_down, down_weight[0]], axis=0))
     resident = jnp.where(swap_flags == 1, (labels + experts // 2) % experts, labels)
     slots_per = step_count * capacity
-    slot_ids = []
-    for step_index in range(step_count):
-        route = placement[step_index]
-        if step_index >= 1:
-            route_hot = (route[:, None] == labels[None, :]).astype(jnp.int32)
-            route = jnp.sum(route_hot * resident[None, :], axis=1)
-        lang_hot = (language[step_index, :, 0][:, None] == labels[None, :]).astype(jnp.int32)
-        target = jnp.sum(lang_hot * route[None, :], axis=1)
-        dest_hot = (target[:, None] == labels[None, :]).astype(jnp.int32)
-        earlier = jnp.cumsum(dest_hot, axis=0) - dest_hot
-        position_in = jnp.sum(earlier * dest_hot, axis=1)
-        slot_ids.append(target * slots_per + step_index * capacity + position_in)
-    slot_id = jnp.concatenate(slot_ids)
+    steps = jnp.arange(step_count, dtype=jnp.int32)
+    placed_hot = placement[:, :, None] == labels[None, None, :]
+    moved = jnp.sum(jnp.where(placed_hot, resident[None, None, :], 0), axis=2)
+    route = jnp.where(steps[:, None] == 0, placement, moved)
+    lang_hot = language[:, :, 0][:, :, None] == labels[None, None, :]
+    target = jnp.sum(jnp.where(lang_hot, route[:, None, :], 0), axis=2)
+    row_ids = jnp.arange(row_count, dtype=jnp.int32)
+    same = (target[:, :, None] == target[:, None, :]) & (row_ids[None, None, :] < row_ids[None, :, None])
+    position_in = jnp.sum(same.astype(jnp.int32), axis=2)
+    slot_id = (target * slots_per + steps[:, None] * capacity + position_in).reshape(-1)
     slot_labels = jnp.arange(experts * slots_per, dtype=jnp.int32)
     select = (slot_id[:, None] == slot_labels[None, :]).astype(jnp.bfloat16)
     rows = states.reshape(step_count * row_count, model_width)

time: 142 us -> 141 us (level)
  no operation moved by 1% of the time
where the time goes in v5:
time: 141 us
  blocking collectives  47.7 us (34%)
  waiting for transfers between devices  41.5 us (29%)
  matrix products  26.2 us (19%)
  starting transfers between devices  15.5 us (11%)
  local copies, waits for them, and re-layouts  6.75 us (5%)
  other arithmetic  2.88 us (2%)
    all_to_all x1, blocking collectives, shards(): lax.all_to_all(served, 'expert', split_axis=0, concat_axis=0, tiled=True)  47.7 us
    all_to_all x1, waiting for transfers between devices, shards(): lax.all_to_all(outgoing, 'expert', split_axis=0, concat_axis=0, tiled=True)  41.5 us
    dot_general x1, matrix products, shards(): update = jnp.dot(hidden, down_full, preferred_element_type=jnp.float32)  21.1 us
    all_to_all x1, starting transfers between devices, shards(): lax.all_to_all(outgoing, 'expert', split_axis=0, concat_axis=0, tiled=True)  15 us
    dot_general x1, matrix products, shards(): jnp.dot(select, returned.reshape(experts * slots_per, model_width), prefe...  2.86 us
  transfers between devices with their start and end apart: 3, of which 1 were waited for; matrix products, arithmetic and copies ran while one was open for 6% of the time, Pallas kernels for 0%

profile of v5, /device:TPU:32, one launch (start us, length us, event | category | flops | bytes accessed | tf_op | source)
XLA Modules:
  0.0 140.7 jit_solution(8078682628136300554)
XLA Ops:
  0.0 0.0 collective-permute-start
  0.0 0.5 collective-permute-start.1
  0.5 0.7 compare_select_fusion.2
  1.2 0.7 copy.9
  1.9 0.9 select_reduce_fusion.1
  2.8 0.8 broadcast_select_fusion
  3.5 0.2 select_reduce_fusion
  3.8 0.2 convert_reduce_fusion
  4.0 0.1 add_bitcast_fusion
  4.1 2.2 %convolution_convert_fusion = bf16[768,1024]{1,0:T(8,128)(2,1)S(1)} fusion(bf16[384,1024]{1,0:T(8,128)(2,1)} %bitcast.17, s32[384]{0:T(512)S(1)} %add_bitcast_fusion), kind=kOutput, calls=%fused_computation.18 | convolution fusion | flops 605061120 | bytes 2360832 | tf_op jit(solution)/shard_map/rs,rd->sd/dot_general | solution.py:35
  6.3 2.1 %reshape.66 = bf16[128,48,128]{2,1,0:T(8,128)(2,1)} reshape(bf16[768,1024]{1,0:T(8,128)(2,1)S(1)} %convolution_convert_fusion) | data formatting | bytes 3145728 | tf_op jit(solution)/shard_map/reshape | solution.py:38
  8.4 15.0 %all-to-all-start = ((bf16[128,48,128]{2,1,0:T(8,128)(2,1)}), bf16[128,48,128]{2,1,0:T(8,128)(2,1)S(1)}, u32[]{:S(2)}, u32[]{:S(2)}) async-start(bf16[128,48,128]{2,1,0:T(8,128)(2,1)} %reshape.66), calls=%async_computation | async-start | bytes 3145728 | tf_op jit(solution)/shard_map/all_to_all | solution.py:39
  23.4 41.5 %all-to-all-done = bf16[128,48,128]{2,1,0:T(8,128)(2,1)S(1)} async-done(((bf16[128,48,128]{2,1,0:T(8,128)(2,1)}), bf16[128,48,128]{2,1,0:T(8,128)(2,1)S(1)}, u32[]{:S(2)}, u32[]{:S(2)}) %all-to-all-start) | async-done | bytes 1572896 | tf_op jit(solution)/shard_map/all_to_all | solution.py:39
  65.0 0.7 reshape.67
  65.7 0.0 collective-permute-done
  65.7 0.0 collective-permute-done.1
  65.7 21.1 %fusion.14 = bf16[768,1024]{1,0:T(8,128)(2,1)} fusion(bf16[2048,1024]{1,0:T(8,128)(2,1)} %collective-permute-done.1, bf16[2048,1024]{1,0:T(8,128)(2,1)} %bitcast.14, pred[]{:T(512)S(6)} %eq.89, bf16[768,1024]{1,0:T(8,128)(2,1)S(1)} %reshape.67, bf16[1024,2048]{1,0:T(8,128)(2,1)} %collective-permute-done, bf16[1024,2048]{1,0:T(8,128)(2,1)} %bitcast.16), kind=kOutput, calls=%fused_computation.17 | convolution fusion | flops 12967477248 | bytes 19922944 | tf_op jit(solution)/shard_map/dot_general | solution.py:44
  86.8 2.5 %reshape.68 = bf16[128,48,128]{2,1,0:T(8,128)(2,1)S(1)} reshape(bf16[768,1024]{1,0:T(8,128)(2,1)} %fusion.14) | data formatting | bytes 3145728 | tf_op jit(solution)/shard_map/reshape | solution.py:45
  89.4 47.7 %all_to_all.10 = bf16[128,48,128]{2,1,0:T(8,128)(2,1)S(1)} all-to-all(bf16[128,48,128]{2,1,0:T(8,128)(2,1)S(1)} %reshape.68), channel_id=1, replica_groups=mesh['dp'=2,'expert'=128] {'expert'}, dimensions={0} | all-to-all | bytes 3145728 | tf_op jit(solution)/shard_map/all_to_all | solution.py:46
  137.1 0.7 reshape.69
  137.8 2.9 %add_convert_fusion = bf16[384,1024]{1,0:T(8,128)(2,1)} fusion(bf16[384,1024]{1,0:T(8,128)(2,1)} %bitcast.18, bf16[768,1024]{1,0:T(8,128)(2,1)S(1)} %reshape.69, s32[384]{0:T(512)S(1)} %add_bitcast_fusion), kind=kOutput, calls=%fused_computation.19 | convolution fusion | flops 605454336 | bytes 3147264 | tf_op jit(solution)/shard_map/dot_general | solution.py:47
  (3 shorter events, 0.0 us)
Async XLA Ops:
  0.0 65.7 %collective-permute-start = (bf16[1024,2048]{1,0:T(8,128)(2,1)}, bf16[1024,2048]{1,0:T(8,128)(2,1)}, u32[]{:S(2)}, u32[]{:S(2)}) collective-permute-start(bf16[1024,2048]{1,0:T(8,128)(2,1)} %bitcast.15), channel_id=1, source_target_pairs={{0,128},{128,0},{1,129},{129,1},{2,130},{130,2},{3,131},{131,3},{4... | collective-permute-start | bytes 12582920 | tf_op jit(solution)/shard_map/ppermute | solution.py:13
  0.0 65.7 %collective-permute-start.1 = (bf16[2048,1024]{1,0:T(8,128)(2,1)}, bf16[2048,1024]{1,0:T(8,128)(2,1)}, u32[]{:S(2)}, u32[]{:S(2)}) collective-permute-start(bf16[2048,1024]{1,0:T(8,128)(2,1)} %bitcast.13), channel_id=1, source_target_pairs={{0,128},{128,0},{1,129},{129,1},{2,130},{130,2},{3,131},{131,3},{4... | collective-permute-start | bytes 12582920 | tf_op jit(solution)/shard_map/ppermute | solution.py:14
  8.4 56.5 %all-to-all-start = ((bf16[128,48,128]{2,1,0:T(8,128)(2,1)}), bf16[128,48,128]{2,1,0:T(8,128)(2,1)S(1)}, u32[]{:S(2)}, u32[]{:S(2)}) async-start(bf16[128,48,128]{2,1,0:T(8,128)(2,1)} %reshape.66), calls=%async_computation | async-start | bytes 3145728 | tf_op jit(solution)/shard_map/all_to_all | solution.py:39

commit v6 on v5

--- a/solution.py
+++ b/solution.py
@@ -12,11 +12,8 @@
     pair = [(0, 1), (1, 0)]
     other_up = lax.ppermute(up_weight[0], "dp", pair)
     other_down = lax.ppermute(down_weight[0], "dp", pair)
-    first = lax.axis_index("dp") == 0
-    up_full = jnp.where(first, jnp.concatenate([up_weight[0], other_up], axis=1),
-                        jnp.concatenate([other_up, up_weight[0]], axis=1))
-    down_full = jnp.where(first, jnp.concatenate([down_weight[0], other_down], axis=0),
-                          jnp.concatenate([other_down, down_weight[0]], axis=0))
+    up_full = jnp.concatenate([up_weight[0], other_up], axis=1)
+    down_full = jnp.concatenate([down_weight[0], other_down], axis=0)
     resident = jnp.where(swap_flags == 1, (labels + experts // 2) % experts, labels)
     slots_per = step_count * capacity
     steps = jnp.arange(step_count, dtype=jnp.int32)

time: 141 us -> 133 us (0.943)
  blocking collectives: 47.7 us -> 104 us
  waiting for transfers between devices: 41.5 us -> 0.01 us
  starting transfers between devices: 15.5 us -> 0.51 us
  matrix products: 26.2 us -> 21.7 us
  local copies, waits for them, and re-layouts: 6.75 us -> 3.55 us
    all_to_all x0 -> x1, blocking collectives: none -> 56.3 us  [shards(): lax.all_to_all(outgoing, 'expert', split_axis=0, concat_axis=0, tiled=True)]
    all_to_all x1 -> x0, waiting for transfers between devices: 41.5 us -> none  [shards(): lax.all_to_all(outgoing, 'expert', split_axis=0, concat_axis=0, tiled=True)]
    all_to_all x1 -> x0, starting transfers between devices: 15 us -> none  [shards(): lax.all_to_all(outgoing, 'expert', split_axis=0, concat_axis=0, tiled=True)]
    dot_general x1, matrix products: 21.1 us -> 16.6 us  [shards(): update = jnp.dot(hidden, down_full, preferred_element_type=jnp.float32)]
    reshape x1, local copies, waits for them, and re-layouts: 2.55 us -> 0.73 us  [shards(): served = update.astype(jnp.bfloat16).reshape(packed)]
  transfers between devices with their start and end apart: 3 -> 2, of which waited for: 1 -> 0; matrix products, arithmetic and copies ran while one was open for 6% -> 5% of each run, Pallas kernels for 0% -> 0%
where the time goes in v6:
time: 133 us
  blocking collectives  104 us (78%)
  matrix products  21.7 us (16%)
  local copies, waits for them, and re-layouts  3.55 us (3%)
  other arithmetic  2.88 us (2%)
    all_to_all x1, blocking collectives, shards(): lax.all_to_all(outgoing, 'expert', split_axis=0, concat_axis=0, tiled=True)  56.3 us
    all_to_all x1, blocking collectives, shards(): lax.all_to_all(served, 'expert', split_axis=0, concat_axis=0, tiled=True)  47.7 us
    dot_general x1, matrix products, shards(): update = jnp.dot(hidden, down_full, preferred_element_type=jnp.float32)  16.6 us
    dot_general x1, matrix products, shards(): jnp.dot(select, returned.reshape(experts * slots_per, model_width), prefe...  2.84 us
  transfers between devices with their start and end apart: 2, of which 0 were waited for; matrix products, arithmetic and copies ran while one was open for 5% of the time, Pallas kernels for 0%

profile of v6, /device:TPU:32, one launch (start us, length us, event | category | flops | bytes accessed | tf_op | source)
XLA Modules:
  0.0 132.7 jit_solution(10979203305801009302)
XLA Ops:
  0.0 0.0 collective-permute-start
  0.0 0.5 collective-permute-start.1
  0.5 0.7 compare_select_fusion.2
  1.2 0.7 copy.9
  1.9 0.9 select_reduce_fusion.1
  2.8 0.8 broadcast_select_fusion
  3.5 0.2 select_reduce_fusion
  3.8 0.2 convert_reduce_fusion
  4.0 0.1 add_bitcast_fusion
  4.1 2.2 %convolution_convert_fusion = bf16[768,1024]{1,0:T(8,128)(2,1)S(1)} fusion(bf16[384,1024]{1,0:T(8,128)(2,1)} %bitcast.17, s32[384]{0:T(512)S(1)} %add_bitcast_fusion), kind=kOutput, calls=%fused_computation.10 | convolution fusion | flops 605061120 | bytes 2360832 | tf_op jit(solution)/shard_map/rs,rd->sd/dot_general | solution.py:32
  6.3 0.7 reshape.66
  7.1 56.3 %all_to_all.10 = bf16[128,48,128]{2,1,0:T(8,128)(2,1)S(1)} all-to-all(bf16[128,48,128]{2,1,0:T(8,128)(2,1)S(1)} %reshape.66), channel_id=1, replica_groups=mesh['dp'=2,'expert'=128] {'expert'}, dimensions={0} | all-to-all | bytes 3145728 | tf_op jit(solution)/shard_map/all_to_all | solution.py:36
  63.4 0.7 reshape.67
  64.1 0.0 collective-permute-done
  64.1 0.0 collective-permute-done.1
  64.1 16.6 %fusion.10 = bf16[768,1024]{1,0:T(8,128)(2,1)S(1)} fusion(bf16[2048,1024]{1,0:T(8,128)(2,1)} %collective-permute-done.1, bf16[2048,1024]{1,0:T(8,128)(2,1)} %bitcast.14, bf16[768,1024]{1,0:T(8,128)(2,1)S(1)} %reshape.67, bf16[1024,2048]{1,0:T(8,128)(2,1)} %collective-permute-done, bf16[1024,2048]{1,0:T(8,128)(2,1)} %bitcast.16), kind=kOutput, calls=%fused_computation.9 | convolution fusion | flops 12925534208 | bytes 19922944 | tf_op jit(solution)/shard_map/dot_general | solution.py:41
  80.7 0.7 reshape.68
  81.5 47.7 %all_to_all.11 = bf16[128,48,128]{2,1,0:T(8,128)(2,1)S(1)} all-to-all(bf16[128,48,128]{2,1,0:T(8,128)(2,1)S(1)} %reshape.68), channel_id=1, replica_groups=mesh['dp'=2,'expert'=128] {'expert'}, dimensions={0} | all-to-all | bytes 3145728 | tf_op jit(solution)/shard_map/all_to_all | solution.py:43
  129.1 0.7 reshape.69
  129.8 2.8 %add_convert_fusion = bf16[384,1024]{1,0:T(8,128)(2,1)} fusion(bf16[384,1024]{1,0:T(8,128)(2,1)} %bitcast.18, bf16[768,1024]{1,0:T(8,128)(2,1)S(1)} %reshape.69, s32[384]{0:T(512)S(1)} %add_bitcast_fusion), kind=kOutput, calls=%fused_computation.11 | convolution fusion | flops 605454336 | bytes 3147264 | tf_op jit(solution)/shard_map/dot_general | solution.py:44
  (3 shorter events, 0.0 us)
Async XLA Ops:
  0.0 64.1 %collective-permute-start = (bf16[1024,2048]{1,0:T(8,128)(2,1)}, bf16[1024,2048]{1,0:T(8,128)(2,1)}, u32[]{:S(2)}, u32[]{:S(2)}) collective-permute-start(bf16[1024,2048]{1,0:T(8,128)(2,1)} %bitcast.15), channel_id=1, source_target_pairs={{0,128},{128,0},{1,129},{129,1},{2,130},{130,2},{3,131},{131,3},{4... | collective-permute-start | bytes 12582920 | tf_op jit(solution)/shard_map/ppermute | solution.py:13
  0.0 64.1 %collective-permute-start.1 = (bf16[2048,1024]{1,0:T(8,128)(2,1)}, bf16[2048,1024]{1,0:T(8,128)(2,1)}, u32[]{:S(2)}, u32[]{:S(2)}) collective-permute-start(bf16[2048,1024]{1,0:T(8,128)(2,1)} %bitcast.13), channel_id=1, source_target_pairs={{0,128},{128,0},{1,129},{129,1},{2,130},{130,2},{3,131},{131,3},{4... | collective-permute-start | bytes 12582920 | tf_op jit(solution)/shard_map/ppermute | solution.py:14

commit v7 on v6

--- a/solution.py
+++ b/solution.py
@@ -1,7 +1,64 @@
 import jax
 import jax.numpy as jnp
 from jax import lax
+from jax.experimental import pallas as pl
+from jax.experimental.pallas import tpu as pltpu
 from jax.sharding import PartitionSpec as P
+
+
+def expert_ffn(rows, up_own, up_other, down_own, down_other, interpret=False):
+    row_count, model_width = rows.shape
+    half = up_own.shape[1]
+    block = 512 if half % 512 == 0 else half
+    blocks = half // block
+
+    def kernel(x_ref, ua_ref, ub_ref, da_ref, db_ref, o_ref, acc_ref):
+        side = pl.program_id(0)
+        chunk = pl.program_id(1)
+
+        @pl.when((side == 0) & (chunk == 0))
+        def _():
+            acc_ref[...] = jnp.zeros_like(acc_ref)
+
+        def accumulate(u_ref, d_ref):
+            hidden = jnp.maximum(
+                jnp.dot(x_ref[...], u_ref[...], preferred_element_type=jnp.float32), 0.0
+            ).astype(jnp.bfloat16)
+            acc_ref[...] += jnp.dot(hidden, d_ref[...], preferred_element_type=jnp.float32)
+
+        @pl.when(side == 0)
+        def _():
+            accumulate(ua_ref, da_ref)
+
+        @pl.when(side == 1)
+        def _():
+            accumulate(ub_ref, db_ref)
+
+        @pl.when((side == 1) & (chunk == blocks - 1))
+        def _():
+            o_ref[...] = acc_ref[...].astype(o_ref.dtype)
+
+    def own(side, chunk):
+        return chunk * (1 - side) + (blocks - 1) * side
+
+    def other(side, chunk):
+        return chunk * side
+
+    return pl.pallas_call(
+        kernel,
+        out_shape=jax.ShapeDtypeStruct((row_count, model_width), jnp.bfloat16),
+        grid=(2, blocks),
+        in_specs=[
+            pl.BlockSpec((row_count, model_width), lambda s, c: (0, 0)),
+            pl.BlockSpec((model_width, block), lambda s, c: (0, own(s, c))),
+            pl.BlockSpec((model_width, block), lambda s, c: (0, other(s, c))),
+            pl.BlockSpec((block, model_width), lambda s, c: (own(s, c), 0)),
+            pl.BlockSpec((block, model_width), lambda s, c: (other(s, c), 0)),
+        ],
+        out_specs=pl.BlockSpec((row_count, model_width), lambda s, c: (0, 0)),
+        scratch_shapes=[pltpu.VMEM((row_count, model_width), jnp.float32)],
+        interpret=interpret,
+    )(rows, up_own, up_other, down_own, down_other)
 
 
 def shards(states, language, placement, swap_flags, up_weight, down_weight):
@@ -12,8 +69,6 @@
     pair = [(0, 1), (1, 0)]
     other_up = lax.ppermute(up_weight[0], "dp", pair)
     other_down = lax.ppermute(down_weight[0], "dp", pair)
-    up_full = jnp.concatenate([up_weight[0], other_up], axis=1)
-    down_full = jnp.concatenate([down_weight[0], other_down], axis=0)
     resident = jnp.where(swap_flags == 1, (labels + experts // 2) % experts, labels)
     slots_per = step_count * capacity
     steps = jnp.arange(step_count, dtype=jnp.int32)
@@ -35,11 +90,8 @@
     outgoing = outgoing.astype(jnp.bfloat16).reshape(packed)
     arrived = lax.all_to_all(outgoing, "expert", split_axis=0, concat_axis=0, tiled=True)
     flat_rows = arrived.reshape(experts * slots_per, model_width)
-    hidden = jnp.maximum(
-        jnp.dot(flat_rows, up_full, preferred_element_type=jnp.float32), 0.0
-    ).astype(jnp.bfloat16)
-    update = jnp.dot(hidden, down_full, preferred_element_type=jnp.float32)
-    served = update.astype(jnp.bfloat16).reshape(packed)
+    update = expert_ffn(flat_rows, up_weight[0], other_up, down_weight[0], other_down)
+    served = update.reshape(packed)
     returned = lax.all_to_all(served, "expert", split_axis=0, concat_axis=0, tiled=True)
     selected = jnp.dot(
         select,

time: 133 us -> 139 us (1.045)
  Pallas kernels: 0 us -> 19.1 us
  matrix products: 21.7 us -> 5.08 us
  local copies, waits for them, and re-layouts: 3.55 us -> 6.76 us
    pallas_call x0 -> x1, Pallas kernels: none -> 19.1 us  [expert_ffn(): pl.pallas_call(kernel, out_shape=jax.ShapeDtypeStruct((row_count, model_w...]
    dot_general x1 -> x0, matrix products: 16.6 us -> none  [shards(): update = jnp.dot(hidden, down_full, preferred_element_type=jnp.float32)]
    reshape x1, local copies, waits for them, and re-layouts: 0.73 us -> 2.55 us  [shards(): served = update.reshape(packed)]
  transfers between devices with their start and end apart: 2 -> 2, of which waited for: 0 -> 0; matrix products, arithmetic and copies ran while one was open for 5% -> 6% of each run, Pallas kernels for 0% -> 0%
where the time goes in v7:
time: 139 us; the launch traced here: 138 us
  blocking collectives  104 us (75%)
  Pallas kernels  19.1 us (14%)
  local copies, waits for them, and re-layouts  6.76 us (5%)
  matrix products  5.08 us (4%)
  other arithmetic  2.88 us (2%)
    all_to_all x1, blocking collectives, shards(): lax.all_to_all(outgoing, 'expert', split_axis=0, concat_axis=0, tiled=True)  56.3 us
    all_to_all x1, blocking collectives, shards(): lax.all_to_all(served, 'expert', split_axis=0, concat_axis=0, tiled=True)  47.7 us
    pallas_call x1, Pallas kernels, expert_ffn(): pl.pallas_call(kernel, out_shape=jax.ShapeDtypeStruct((row_count, model_w...  19.1 us
    dot_general x1, matrix products, shards(): jnp.dot(select, returned.reshape(experts * slots_per, model_width), prefe...  2.84 us
  transfers between devices with their start and end apart: 2, of which 0 were waited for; matrix products, arithmetic and copies ran while one was open for 6% of the time, Pallas kernels for 0%

profile of v7, /device:TPU:32, one launch (start us, length us, event | category | flops | bytes accessed | tf_op | source)
XLA Modules:
  0.0 138.4 jit_solution(1552478981997255796)
XLA Ops:
  0.0 0.0 collective-permute-start
  0.0 0.5 collective-permute-start.1
  0.5 0.7 compare_select_fusion.2
  1.2 0.7 copy.9
  1.9 0.9 select_reduce_fusion.1
  2.8 0.8 broadcast_select_fusion
  3.5 0.2 select_reduce_fusion
  3.8 0.2 convert_reduce_fusion
  4.0 0.1 add_bitcast_fusion
  4.1 2.2 %convolution_convert_fusion = bf16[768,1024]{1,0:T(8,128)(2,1)S(1)} fusion(bf16[384,1024]{1,0:T(8,128)(2,1)} %bitcast.16, s32[384]{0:T(512)S(1)} %add_bitcast_fusion), kind=kOutput, calls=%fused_computation | convolution fusion | flops 605061120 | bytes 2360832 | tf_op jit(solution)/shard_map/rs,rd->sd/dot_general | solution.py:87
  6.3 0.7 reshape.66
  7.1 56.3 %all_to_all.10 = bf16[128,48,128]{2,1,0:T(8,128)(2,1)S(1)} all-to-all(bf16[128,48,128]{2,1,0:T(8,128)(2,1)S(1)} %reshape.66), channel_id=1, replica_groups=mesh['dp'=2,'expert'=128] {'expert'}, dimensions={0} | all-to-all | bytes 3145728 | tf_op jit(solution)/shard_map/all_to_all | solution.py:91
  63.4 2.1 %reshape.67.x_ref = bf16[768,1024]{1,0:T(8,128)(2,1)} reshape(bf16[128,48,128]{2,1,0:T(8,128)(2,1)S(1)} %all_to_all.10) | data formatting | bytes 3145728 | tf_op jit(solution)/shard_map/reshape | solution.py:92
  65.5 0.0 collective-permute-done.ub_ref
  65.5 0.0 collective-permute-done.1.db_ref
  65.5 19.1 %shard_map.64 = bf16[768,1024]{1,0:T(8,128)(2,1)} custom-call(bf16[768,1024]{1,0:T(8,128)(2,1)} %reshape.67.x_ref, bf16[1024,2048]{1,0:T(8,128)(2,1)} %bitcast.12, bf16[1024,2048]{1,0:T(8,128)(2,1)} %collective-permute-done.ub_ref, bf16[2048,1024]{1,0:T(8,128)(2,1)} %bitcast.14, bf16[2048,1024]{1,0:T(8,128)(2,1)} %collective-permute-done.1.db_ref), custom_call_target="tpu_custom_call" | custom-call | tf_op jit(solution)/shard_map/pallas_call | solution.py:47
  84.6 2.5 %reshape.68 = bf16[128,48,128]{2,1,0:T(8,128)(2,1)S(1)} reshape(bf16[768,1024]{1,0:T(8,128)(2,1)} %shard_map.64) | data formatting | bytes 3145728 | tf_op jit(solution)/shard_map/reshape | solution.py:94
  87.2 47.7 %all_to_all.11 = bf16[128,48,128]{2,1,0:T(8,128)(2,1)S(1)} all-to-all(bf16[128,48,128]{2,1,0:T(8,128)(2,1)S(1)} %reshape.68), channel_id=1, replica_groups=mesh['dp'=2,'expert'=128] {'expert'}, dimensions={0} | all-to-all | bytes 3145728 | tf_op jit(solution)/shard_map/all_to_all | solution.py:95
  134.9 0.7 reshape.69
  135.6 2.8 %add_convert_fusion = bf16[384,1024]{1,0:T(8,128)(2,1)} fusion(bf16[384,1024]{1,0:T(8,128)(2,1)} %bitcast.17, bf16[768,1024]{1,0:T(8,128)(2,1)S(1)} %reshape.69, s32[384]{0:T(512)S(1)} %add_bitcast_fusion), kind=kOutput, calls=%fused_computation.1 | convolution fusion | flops 605454336 | bytes 3147264 | tf_op jit(solution)/shard_map/dot_general | solution.py:96
  (3 shorter events, 0.0 us)
Async XLA Ops:
  0.0 65.5 %collective-permute-start = (bf16[1024,2048]{1,0:T(8,128)(2,1)}, bf16[1024,2048]{1,0:T(8,128)(2,1)}, u32[]{:S(2)}, u32[]{:S(2)}) collective-permute-start(bf16[1024,2048]{1,0:T(8,128)(2,1)} %bitcast.11), channel_id=1, source_target_pairs={{0,128},{128,0},{1,129},{129,1},{2,130},{130,2},{3,131},{131,3},{4... | collective-permute-start | bytes 12582920 | tf_op jit(solution)/shard_map/ppermute | solution.py:70
  0.0 65.5 %collective-permute-start.1 = (bf16[2048,1024]{1,0:T(8,128)(2,1)}, bf16[2048,1024]{1,0:T(8,128)(2,1)}, u32[]{:S(2)}, u32[]{:S(2)}) collective-permute-start(bf16[2048,1024]{1,0:T(8,128)(2,1)} %bitcast.13), channel_id=1, source_target_pairs={{0,128},{128,0},{1,129},{129,1},{2,130},{130,2},{3,131},{131,3},{4... | collective-permute-start | bytes 12582920 | tf_op jit(solution)/shard_map/ppermute | solution.py:71

commit v8 on v6

--- a/solution.py
+++ b/solution.py
@@ -41,11 +41,7 @@
     update = jnp.dot(hidden, down_full, preferred_element_type=jnp.float32)
     served = update.astype(jnp.bfloat16).reshape(packed)
     returned = lax.all_to_all(served, "expert", split_axis=0, concat_axis=0, tiled=True)
-    selected = jnp.dot(
-        select,
-        returned.reshape(experts * slots_per, model_width),
-        preferred_element_type=jnp.float32,
-    )
+    selected = jnp.take(returned.reshape(experts * slots_per, model_width), slot_id, axis=0)
     updated = (rows.astype(jnp.float32) + selected).astype(jnp.bfloat16)
     return updated.reshape(step_count, row_count, model_width)
 

time: 133 us -> 135 us (1.015)
  blocking collectives: 104 us -> 56.3 us
  waiting for transfers between devices: 0.01 us -> 40.8 us
  starting transfers between devices: 0.51 us -> 7.53 us
  local copies, waits for them, and re-layouts: 3.55 us -> 6.98 us
  matrix products: 21.7 us -> 18.9 us
    all_to_all x1 -> x0, blocking collectives: 47.7 us -> none  [shards(): lax.all_to_all(served, 'expert', split_axis=0, concat_axis=0, tiled=True)]
    all_to_all x0 -> x1, waiting for transfers between devices: none -> 40.8 us  [shards(): lax.all_to_all(served, 'expert', split_axis=0, concat_axis=0, tiled=True)]
    all_to_all x0 -> x1, starting transfers between devices: none -> 7.02 us  [shards(): lax.all_to_all(served, 'expert', split_axis=0, concat_axis=0, tiled=True)]
    dot_general x1 -> x0, matrix products: 2.84 us -> none  [shards(): jnp.dot(select, returned.reshape(experts * slots_per, model_width), prefe...]
    gather x0 -> x1, local copies, waits for them, and re-layouts: none -> 2.07 us  [shards(): jnp.take(returned.reshape(experts * slots_per, model_width), slot_id, axi...]
  transfers between devices with their start and end apart: 2 -> 3, of which waited for: 0 -> 1; matrix products, arithmetic and copies ran while one was open for 5% -> 5% of each run, Pallas kernels for 0% -> 0%
where the time goes in v8:
time: 135 us
  blocking collectives  56.3 us (42%)
  waiting for transfers between devices  40.8 us (30%)
  matrix products  18.9 us (14%)
  starting transfers between devices  7.53 us (6%)
  local copies, waits for them, and re-layouts  6.98 us (5%)
  other arithmetic  4.1 us (3%)
    all_to_all x1, blocking collectives, shards(): lax.all_to_all(outgoing, 'expert', split_axis=0, concat_axis=0, tiled=True)  56.3 us
    all_to_all x1, waiting for transfers between devices, shards(): lax.all_to_all(served, 'expert', split_axis=0, concat_axis=0, tiled=True)  40.8 us
    dot_general x1, matrix products, shards(): update = jnp.dot(hidden, down_full, preferred_element_type=jnp.float32)  16.6 us
    all_to_all x1, starting transfers between devices, shards(): lax.all_to_all(served, 'expert', split_axis=0, concat_axis=0, tiled=True)  7.02 us
  transfers between devices with their start and end apart: 3, of which 1 were waited for; matrix products, arithmetic and copies ran while one was open for 5% of the time, Pallas kernels for 0%

profile of v8, /device:TPU:32, one launch (start us, length us, event | category | flops | bytes accessed | tf_op | source)
XLA Modules:
  0.0 134.7 jit_solution(14098751118987528319)
XLA Ops:
  0.0 0.0 collective-permute-start
  0.0 0.5 collective-permute-start.1
  0.5 0.7 compare_select_fusion.4
  1.2 0.7 copy.11
  1.9 0.9 select_reduce_fusion.1
  2.8 0.8 broadcast_select_fusion
  3.5 0.2 select_reduce_fusion
  3.8 0.2 convert_reduce_fusion
  4.0 0.1 compare_and_fusion
  4.1 2.2 %convolution_convert_fusion = bf16[768,1024]{1,0:T(8,128)(2,1)S(1)} fusion(bf16[384,1024]{1,0:T(8,128)(2,1)} %bitcast.16, s32[384]{0:T(512)S(1)} %bitcast.18), kind=kOutput, calls=%fused_computation.11 | convolution fusion | flops 605061120 | bytes 2360832 | tf_op jit(solution)/shard_map/rs,rd->sd/dot_general | solution.py:32
  6.3 0.7 reshape.120
  7.1 56.3 %all_to_all.10 = bf16[128,48,128]{2,1,0:T(8,128)(2,1)S(1)} all-to-all(bf16[128,48,128]{2,1,0:T(8,128)(2,1)S(1)} %reshape.120), channel_id=1, replica_groups=mesh['dp'=2,'expert'=128] {'expert'}, dimensions={0} | all-to-all | bytes 3145728 | tf_op jit(solution)/shard_map/all_to_all | solution.py:36
  63.4 0.7 reshape.121
  64.1 0.0 collective-permute-done
  64.1 0.0 collective-permute-done.1
  64.1 16.6 %fusion.10 = bf16[768,1024]{1,0:T(8,128)(2,1)S(1)} fusion(bf16[2048,1024]{1,0:T(8,128)(2,1)} %collective-permute-done.1, bf16[2048,1024]{1,0:T(8,128)(2,1)} %bitcast.21, bf16[768,1024]{1,0:T(8,128)(2,1)S(1)} %reshape.121, bf16[1024,2048]{1,0:T(8,128)(2,1)} %collective-permute-done, bf16[1024,2048]{1,0:T(8,128)(2,1)} %bitcast.23), kind=kOutput, calls=%fused_computation.10 | convolution fusion | flops 12925534208 | bytes 19922944 | tf_op jit(solution)/shard_map/dot_general | solution.py:41
  80.8 2.1 %reshape.122 = bf16[128,48,128]{2,1,0:T(8,128)(2,1)} reshape(bf16[768,1024]{1,0:T(8,128)(2,1)S(1)} %fusion.10) | data formatting | bytes 3145728 | tf_op jit(solution)/shard_map/reshape | solution.py:42
  82.9 7.0 %all-to-all-start.1 = ((bf16[128,48,128]{2,1,0:T(8,128)(2,1)}), bf16[128,48,128]{2,1,0:T(8,128)(2,1)S(1)}, u32[]{:S(2)}, u32[]{:S(2)}) async-start(bf16[128,48,128]{2,1,0:T(8,128)(2,1)} %reshape.122), calls=%async_computation.1 | async-start | bytes 3145728 | tf_op jit(solution)/shard_map/all_to_all | solution.py:43
  89.9 40.8 %all-to-all-done.1 = bf16[128,48,128]{2,1,0:T(8,128)(2,1)S(1)} async-done(((bf16[128,48,128]{2,1,0:T(8,128)(2,1)}), bf16[128,48,128]{2,1,0:T(8,128)(2,1)S(1)}, u32[]{:S(2)}, u32[]{:S(2)}) %all-to-all-start.1) | async-done | bytes 1572896 | tf_op jit(solution)/shard_map/all_to_all | solution.py:43
  130.7 0.7 reshape.123
  131.5 0.0 copy-start
  131.5 2.1 %gather_fusion = bf16[384,1024]{1,0:T(8,128)(2,1)S(1)} fusion(bf16[768,1024]{1,0:T(8,128)(2,1)S(1)} %reshape.123, s32[1024]{0:T(1024)S(1)} %pad_clamp_fusion), kind=kCustom, calls=%fused_computation | custom fusion | bytes 1574400 | tf_op jit(solution)/shard_map/jit(_take)/gather | solution.py:44
  133.5 0.0 copy-done
  133.6 1.2 add_convert_fusion
  (5 shorter events, 0.1 us)
Async XLA Ops:
  0.0 64.1 %collective-permute-start = (bf16[1024,2048]{1,0:T(8,128)(2,1)}, bf16[1024,2048]{1,0:T(8,128)(2,1)}, u32[]{:S(2)}, u32[]{:S(2)}) collective-permute-start(bf16[1024,2048]{1,0:T(8,128)(2,1)} %bitcast.22), channel_id=1, source_target_pairs={{0,128},{128,0},{1,129},{129,1},{2,130},{130,2},{3,131},{131,3},{4... | collective-permute-start | bytes 12582920 | tf_op jit(solution)/shard_map/ppermute | solution.py:13
  0.0 64.1 %collective-permute-start.1 = (bf16[2048,1024]{1,0:T(8,128)(2,1)}, bf16[2048,1024]{1,0:T(8,128)(2,1)}, u32[]{:S(2)}, u32[]{:S(2)}) collective-permute-start(bf16[2048,1024]{1,0:T(8,128)(2,1)} %bitcast.20), channel_id=1, source_target_pairs={{0,128},{128,0},{1,129},{129,1},{2,130},{130,2},{3,131},{131,3},{4... | collective-permute-start | bytes 12582920 | tf_op jit(solution)/shard_map/ppermute | solution.py:14
  82.9 47.9 %all-to-all-start.1 = ((bf16[128,48,128]{2,1,0:T(8,128)(2,1)}), bf16[128,48,128]{2,1,0:T(8,128)(2,1)S(1)}, u32[]{:S(2)}, u32[]{:S(2)}) async-start(bf16[128,48,128]{2,1,0:T(8,128)(2,1)} %reshape.122), calls=%async_computation.1 | async-start | bytes 3145728 | tf_op jit(solution)/shard_map/all_to_all | solution.py:43
  131.5 2.1 %copy-start = (bf16[3,128,1024]{2,1,0:T(8,128)(2,1)S(1)}, bf16[3,128,1024]{2,1,0:T(8,128)(2,1)}, u32[]{:S(2)}) copy-start(bf16[3,128,1024]{2,1,0:T(8,128)(2,1)} %param.6) | copy-start | bytes 2359300

commit v9 on v6

--- a/solution.py
+++ b/solution.py
@@ -14,12 +14,12 @@
     other_down = lax.ppermute(down_weight[0], "dp", pair)
     up_full = jnp.concatenate([up_weight[0], other_up], axis=1)
     down_full = jnp.concatenate([down_weight[0], other_down], axis=0)
-    resident = jnp.where(swap_flags == 1, (labels + experts // 2) % experts, labels)
     slots_per = step_count * capacity
     steps = jnp.arange(step_count, dtype=jnp.int32)
     placed_hot = placement[:, :, None] == labels[None, None, :]
-    moved = jnp.sum(jnp.where(placed_hot, resident[None, None, :], 0), axis=2)
-    route = jnp.where(steps[:, None] == 0, placement, moved)
+    flag_at = jnp.sum(jnp.where(placed_hot, swap_flags[None, None, :], 0), axis=2)
+    swapped = (steps[:, None] >= 1) & (flag_at == 1)
+    route = jnp.where(swapped, (placement + experts // 2) % experts, placement)
     lang_hot = language[:, :, 0][:, :, None] == labels[None, None, :]
     target = jnp.sum(jnp.where(lang_hot, route[:, None, :], 0), axis=2)
     row_ids = jnp.arange(row_count, dtype=jnp.int32)

time: 133 us -> 132 us (level)
  no operation moved by 1% of the time
where the time goes in v9:
time: 132 us
  blocking collectives  104 us (79%)
  matrix products  21.7 us (16%)
  local copies, waits for them, and re-layouts  3.56 us (3%)
  other arithmetic  2.23 us (2%)
    all_to_all x1, blocking collectives, shards(): lax.all_to_all(outgoing, 'expert', split_axis=0, concat_axis=0, tiled=True)  56.3 us
    all_to_all x1, blocking collectives, shards(): lax.all_to_all(served, 'expert', split_axis=0, concat_axis=0, tiled=True)  47.7 us
    dot_general x1, matrix products, shards(): update = jnp.dot(hidden, down_full, preferred_element_type=jnp.float32)  16.6 us
    dot_general x1, matrix products, shards(): jnp.dot(select, returned.reshape(experts * slots_per, model_width), prefe...  2.84 us
  transfers between devices with their start and end apart: 2, of which 0 were waited for; matrix products, arithmetic and copies ran while one was open for 5% of the time, Pallas kernels for 0%

profile of v9, /device:TPU:32, one launch (start us, length us, event | category | flops | bytes accessed | tf_op | source)
XLA Modules:
  0.0 132.1 jit_solution(15218993811036922155)
XLA Ops:
  0.0 0.0 collective-permute-start
  0.0 0.5 collective-permute-start.1
  0.5 0.7 copy.9
  1.2 0.9 select_reduce_fusion.1
  2.2 0.8 fusion.18
  2.9 0.2 select_reduce_fusion
  3.1 0.2 convert_reduce_fusion
  3.4 0.1 add_bitcast_fusion
  3.4 2.2 %convolution_convert_fusion = bf16[768,1024]{1,0:T(8,128)(2,1)S(1)} fusion(bf16[384,1024]{1,0:T(8,128)(2,1)} %bitcast.17, s32[384]{0:T(512)S(1)} %add_bitcast_fusion), kind=kOutput, calls=%fused_computation.10 | convolution fusion | flops 605061120 | bytes 2360832 | tf_op jit(solution)/shard_map/rs,rd->sd/dot_general | solution.py:32
  5.7 0.7 reshape.66
  6.4 56.3 %all_to_all.10 = bf16[128,48,128]{2,1,0:T(8,128)(2,1)S(1)} all-to-all(bf16[128,48,128]{2,1,0:T(8,128)(2,1)S(1)} %reshape.66), channel_id=1, replica_groups=mesh['dp'=2,'expert'=128] {'expert'}, dimensions={0} | all-to-all | bytes 3145728 | tf_op jit(solution)/shard_map/all_to_all | solution.py:36
  62.8 0.7 reshape.67
  63.5 0.0 collective-permute-done
  63.5 0.0 collective-permute-done.1
  63.5 16.6 %fusion.10 = bf16[768,1024]{1,0:T(8,128)(2,1)S(1)} fusion(bf16[2048,1024]{1,0:T(8,128)(2,1)} %collective-permute-done.1, bf16[2048,1024]{1,0:T(8,128)(2,1)} %bitcast.14, bf16[768,1024]{1,0:T(8,128)(2,1)S(1)} %reshape.67, bf16[1024,2048]{1,0:T(8,128)(2,1)} %collective-permute-done, bf16[1024,2048]{1,0:T(8,128)(2,1)} %bitcast.16), kind=kOutput, calls=%fused_computation.9 | convolution fusion | flops 12925534208 | bytes 19922944 | tf_op jit(solution)/shard_map/dot_general | solution.py:41
  80.1 0.7 reshape.68
  80.8 47.7 %all_to_all.11 = bf16[128,48,128]{2,1,0:T(8,128)(2,1)S(1)} all-to-all(bf16[128,48,128]{2,1,0:T(8,128)(2,1)S(1)} %reshape.68), channel_id=1, replica_groups=mesh['dp'=2,'expert'=128] {'expert'}, dimensions={0} | all-to-all | bytes 3145728 | tf_op jit(solution)/shard_map/all_to_all | solution.py:43
  128.5 0.7 reshape.69
  129.2 2.8 %add_convert_fusion = bf16[384,1024]{1,0:T(8,128)(2,1)} fusion(bf16[384,1024]{1,0:T(8,128)(2,1)} %bitcast.18, bf16[768,1024]{1,0:T(8,128)(2,1)S(1)} %reshape.69, s32[384]{0:T(512)S(1)} %add_bitcast_fusion), kind=kOutput, calls=%fused_computation.11 | convolution fusion | flops 605454336 | bytes 3147264 | tf_op jit(solution)/shard_map/dot_general | solution.py:44
  (3 shorter events, 0.0 us)
Async XLA Ops:
  0.0 63.5 %collective-permute-start = (bf16[1024,2048]{1,0:T(8,128)(2,1)}, bf16[1024,2048]{1,0:T(8,128)(2,1)}, u32[]{:S(2)}, u32[]{:S(2)}) collective-permute-start(bf16[1024,2048]{1,0:T(8,128)(2,1)} %bitcast.15), channel_id=1, source_target_pairs={{0,128},{128,0},{1,129},{129,1},{2,130},{130,2},{3,131},{131,3},{4... | collective-permute-start | bytes 12582920 | tf_op jit(solution)/shard_map/ppermute | solution.py:13
  0.0 63.5 %collective-permute-start.1 = (bf16[2048,1024]{1,0:T(8,128)(2,1)}, bf16[2048,1024]{1,0:T(8,128)(2,1)}, u32[]{:S(2)}, u32[]{:S(2)}) collective-permute-start(bf16[2048,1024]{1,0:T(8,128)(2,1)} %bitcast.13), channel_id=1, source_target_pairs={{0,128},{128,0},{1,129},{129,1},{2,130},{130,2},{3,131},{131,3},{4... | collective-permute-start | bytes 12582920 | tf_op jit(solution)/shard_map/ppermute | solution.py:14

commit v10 on v9

--- a/solution.py
+++ b/solution.py
@@ -9,11 +9,6 @@
     experts = lax.axis_size("expert")
     capacity = max(2, 2 * row_count // experts)
     labels = jnp.arange(experts, dtype=jnp.int32)
-    pair = [(0, 1), (1, 0)]
-    other_up = lax.ppermute(up_weight[0], "dp", pair)
-    other_down = lax.ppermute(down_weight[0], "dp", pair)
-    up_full = jnp.concatenate([up_weight[0], other_up], axis=1)
-    down_full = jnp.concatenate([down_weight[0], other_down], axis=0)
     slots_per = step_count * capacity
     steps = jnp.arange(step_count, dtype=jnp.int32)
     placed_hot = placement[:, :, None] == labels[None, None, :]
@@ -35,10 +30,22 @@
     outgoing = outgoing.astype(jnp.bfloat16).reshape(packed)
     arrived = lax.all_to_all(outgoing, "expert", split_axis=0, concat_axis=0, tiled=True)
     flat_rows = arrived.reshape(experts * slots_per, model_width)
-    hidden = jnp.maximum(
-        jnp.dot(flat_rows, up_full, preferred_element_type=jnp.float32), 0.0
-    ).astype(jnp.bfloat16)
-    update = jnp.dot(hidden, down_full, preferred_element_type=jnp.float32)
+    pair = [(0, 1), (1, 0)]
+    other_rows = lax.ppermute(flat_rows, "dp", pair)
+
+    def half_ffn(x):
+        hidden = jnp.maximum(
+            jnp.dot(x, up_weight[0], preferred_element_type=jnp.float32), 0.0
+        ).astype(jnp.bfloat16)
+        return jnp.dot(hidden, down_weight[0], preferred_element_type=jnp.float32)
+
+    own_part = half_ffn(flat_rows)
+    split = other_rows.shape[0] // 2
+    sent_back = [
+        lax.ppermute(half_ffn(other_rows[:split]), "dp", pair),
+        lax.ppermute(half_ffn(other_rows[split:]), "dp", pair),
+    ]
+    update = own_part + jnp.concatenate(sent_back, axis=0)
     served = update.astype(jnp.bfloat16).reshape(packed)
     returned = lax.all_to_all(served, "expert", split_axis=0, concat_axis=0, tiled=True)
     selected = jnp.dot(

time: 132 us -> 149 us (1.13)
  matrix products: 21.7 us -> 32.2 us
  waiting for transfers between devices: 0.01 us -> 3.4 us
  local copies, waits for them, and re-layouts: 3.56 us -> 5.85 us
    dot_general x1 -> x4, matrix products: 16.6 us -> 27.1 us  [the longest x3 21.1 us: half_ffn(): return jnp.dot(hidden, down_weight[0], preferred_element_type=jnp.float32)]
    ppermute x2 -> x3, waiting for transfers between devices: 0.01 us -> 3.4 us  [the longest x1 3.4 us: shards(): other_rows = lax.ppermute(flat_rows, 'dp', pair)]
    unnamed x1 -> x7, local copies, waits for them, and re-layouts: 0.68 us -> 2.97 us
  transfers between devices with their start and end apart: 2 -> 3, of which waited for: 0 -> 1; matrix products, arithmetic and copies ran while one was open for 5% -> 10% of each run, Pallas kernels for 0% -> 0%
where the time goes in v10:
time: 149 us
  blocking collectives  105 us (70%)
  matrix products  32.2 us (22%)
  local copies, waits for them, and re-layouts  5.85 us (4%)
  waiting for transfers between devices  3.4 us (2%)
  other arithmetic  2.24 us (2%)
    all_to_all x1, blocking collectives, shards(): lax.all_to_all(outgoing, 'expert', split_axis=0, concat_axis=0, tiled=True)  55.9 us
    all_to_all x1, blocking collectives, shards(): lax.all_to_all(served, 'expert', split_axis=0, concat_axis=0, tiled=True)  48.8 us
    dot_general x3, matrix products, half_ffn(): return jnp.dot(hidden, down_weight[0], preferred_element_type=jnp.float32)  21.1 us
    dot_general x1, matrix products, half_ffn(): jnp.dot(x, up_weight[0], preferred_element_type=jnp.float32)  6.03 us
    ppermute x1, waiting for transfers between devices, shards(): other_rows = lax.ppermute(flat_rows, 'dp', pair)  3.4 us
  transfers between devices with their start and end apart: 3, of which 1 were waited for; matrix products, arithmetic and copies ran while one was open for 10% of the time, Pallas kernels for 0%

profile of v10, /device:TPU:32, one launch (start us, length us, event | category | flops | bytes accessed | tf_op | source)
XLA Modules:
  0.0 149.0 jit_solution(8412233216659630927)
XLA Ops:
  0.0 0.7 copy.9
  0.7 0.9 select_reduce_fusion.1
  1.6 0.8 fusion.32
  2.4 0.2 select_reduce_fusion
  2.6 0.2 convert_reduce_fusion
  2.9 0.1 add_bitcast_fusion
  2.9 2.2 %convolution_convert_fusion = bf16[768,1024]{1,0:T(8,128)(2,1)S(1)} fusion(bf16[384,1024]{1,0:T(8,128)(2,1)} %bitcast.38, s32[384]{0:T(512)S(1)} %add_bitcast_fusion), kind=kOutput, calls=%fused_computation.17 | convolution fusion | flops 605061120 | bytes 2360832 | tf_op jit(solution)/shard_map/rs,rd->sd/dot_general | solution.py:27
  5.2 0.7 reshape.66
  5.9 55.9 %all_to_all.10 = bf16[128,48,128]{2,1,0:T(8,128)(2,1)S(1)} all-to-all(bf16[128,48,128]{2,1,0:T(8,128)(2,1)S(1)} %reshape.66), channel_id=1, replica_groups=mesh['dp'=2,'expert'=128] {'expert'}, dimensions={0} | all-to-all | bytes 3145728 | tf_op jit(solution)/shard_map/all_to_all | solution.py:31
  61.8 0.7 reshape.67
  62.5 0.1 collective-permute-start
  62.6 3.4 %collective-permute-done = bf16[768,1024]{1,0:T(8,128)(2,1)S(1)} collective-permute-done((bf16[768,1024]{1,0:T(8,128)(2,1)S(1)}, bf16[768,1024]{1,0:T(8,128)(2,1)S(1)}, u32[]{:S(2)}, u32[]{:S(2)}) %collective-permute-start) | collective-permute-done | bytes 1572896 | tf_op jit(solution)/shard_map/ppermute | solution.py:34
  66.0 0.0 copy-start.2
  66.0 1.1 copy-done.2
  67.1 8.0 %fusion.2 = f32[384,1024]{1,0:T(8,128)} fusion(bf16[1,2048,1024]{2,1,0:T(8,128)(2,1)} %param.11, bf16[1,1024,2048]{2,1,0:T(8,128)(2,1)} %param.10, bf16[768,1024]{1,0:T(8,128)(2,1)S(1)} %collective-permute-done), kind=kOutput, calls=%fused_computation.3 | convolution fusion | flops 3222798336 | bytes 10747904 | tf_op jit(solution)/shard_map/dot_general | solution.py:40
  75.2 0.1 collective-permute-start.1
  75.3 8.3 %fusion = f32[384,1024]{1,0:T(8,128)} fusion(bf16[1,2048,1024]{2,1,0:T(8,128)(2,1)} %param.11, bf16[1,1024,2048]{2,1,0:T(8,128)(2,1)} %param.10, bf16[768,1024]{1,0:T(8,128)(2,1)} %copy-done.2), kind=kOutput, calls=%fused_computation.1 | convolution fusion | flops 3222798336 | bytes 10747904 | tf_op jit(solution)/shard_map/dot_general | solution.py:40
  83.6 0.0 copy-start
  83.6 0.4 collective-permute-start.2
  83.9 6.0 %maximum_convert_fusion = bf16[768,2048]{1,0:T(8,128)(2,1)S(1)} fusion(bf16[768,1024]{1,0:T(8,128)(2,1)S(1)} %reshape.67, bf16[1,1024,2048]{2,1,0:T(8,128)(2,1)} %param.10), kind=kOutput, calls=%fused_computation | convolution fusion | flops 3224371200 | bytes 8912896 | tf_op jit(solution)/shard_map/dot_general | solution.py:38
  90.0 0.0 collective-permute-done.1
  90.0 0.0 copy-start.1
  90.0 1.1 copy-done.1
  91.1 0.0 collective-permute-done.2
  91.1 0.0 copy-done
  91.1 4.8 %fusion.14 = bf16[768,1024]{1,0:T(8,128)(2,1)S(1)} fusion(f32[384,1024]{1,0:T(8,128)S(1)} %collective-permute-done.2, f32[384,1024]{1,0:T(8,128)} %copy-done.1, bf16[768,2048]{1,0:T(8,128)(2,1)S(1)} %maximum_convert_fusion, bf16[1,2048,1024]{2,1,0:T(8,128)(2,1)S(1)} %copy-done), kind=kOutput, calls=%fused_computation.14 | convolution fusion | flops 3223584768 | bytes 12058624 | tf_op jit(solution)/shard_map/dot_general | solution.py:40
  95.9 0.7 reshape.68
  96.7 48.8 %all_to_all.11 = bf16[128,48,128]{2,1,0:T(8,128)(2,1)S(1)} all-to-all(bf16[128,48,128]{2,1,0:T(8,128)(2,1)S(1)} %reshape.68), channel_id=1, replica_groups=mesh['dp'=2,'expert'=128] {'expert'}, dimensions={0} | all-to-all | bytes 3145728 | tf_op jit(solution)/shard_map/all_to_all | solution.py:50
  145.4 0.7 reshape.69
  146.1 2.9 %add_convert_fusion = bf16[384,1024]{1,0:T(8,128)(2,1)} fusion(bf16[384,1024]{1,0:T(8,128)(2,1)} %bitcast.39, bf16[768,1024]{1,0:T(8,128)(2,1)S(1)} %reshape.69, s32[384]{0:T(512)S(1)} %add_bitcast_fusion), kind=kOutput, calls=%fused_computation.18 | convolution fusion | flops 605454336 | bytes 3147264 | tf_op jit(solution)/shard_map/dot_general | solution.py:51
  (3 shorter events, 0.0 us)
Async XLA Ops:
  62.5 3.5 %collective-permute-start = (bf16[768,1024]{1,0:T(8,128)(2,1)S(1)}, bf16[768,1024]{1,0:T(8,128)(2,1)S(1)}, u32[]{:S(2)}, u32[]{:S(2)}) collective-permute-start(bf16[768,1024]{1,0:T(8,128)(2,1)S(1)} %reshape.67), channel_id=1, source_target_pairs={{0,128},{128,0},{1,129},{129,1},{2,130},{130,2},{3,131},{131,3},{4... | collective-permute-start | bytes 4718600 | tf_op jit(solution)/shard_map/ppermute | solution.py:34
  66.0 1.1 copy-start.2
  75.2 14.8 %collective-permute-start.1 = (f32[384,1024]{1,0:T(8,128)}, f32[384,1024]{1,0:T(8,128)S(1)}, u32[]{:S(2)}, u32[]{:S(2)}) collective-permute-start(f32[384,1024]{1,0:T(8,128)} %fusion.2), channel_id=1, source_target_pairs={{0,128},{128,0},{1,129},{129,1},{2,130},{130,2},{3,131},{131,3},{4... | collective-permute-start | bytes 4718600 | tf_op jit(solution)/shard_map/ppermute | solution.py:45
  83.6 7.6 %copy-start = (bf16[1,2048,1024]{2,1,0:T(8,128)(2,1)S(1)}, bf16[1,2048,1024]{2,1,0:T(8,128)(2,1)}, u32[]{:S(2)}) copy-start(bf16[1,2048,1024]{2,1,0:T(8,128)(2,1)} %param.11) | copy-start | bytes 12582916
  83.6 7.6 %collective-permute-start.2 = (f32[384,1024]{1,0:T(8,128)}, f32[384,1024]{1,0:T(8,128)S(1)}, u32[]{:S(2)}, u32[]{:S(2)}) collective-permute-start(f32[384,1024]{1,0:T(8,128)} %fusion), channel_id=1, source_target_pairs={{0,128},{128,0},{1,129},{129,1},{2,130},{130,2},{3,131},{131,3},{4... | collective-permute-start | bytes 4718600 | tf_op jit(solution)/shard_map/ppermute | solution.py:46
  90.0 1.1 copy-start.1

commit v11 on v9

--- a/solution.py
+++ b/solution.py
@@ -39,14 +39,15 @@
         jnp.dot(flat_rows, up_full, preferred_element_type=jnp.float32), 0.0
     ).astype(jnp.bfloat16)
     update = jnp.dot(hidden, down_full, preferred_element_type=jnp.float32)
-    served = update.astype(jnp.bfloat16).reshape(packed)
+    update = update.astype(jnp.bfloat16).astype(jnp.float32)
+    served = (flat_rows.astype(jnp.float32) + update).astype(jnp.bfloat16).reshape(packed)
     returned = lax.all_to_all(served, "expert", split_axis=0, concat_axis=0, tiled=True)
     selected = jnp.dot(
         select,
         returned.reshape(experts * slots_per, model_width),
         preferred_element_type=jnp.float32,
     )
-    updated = (rows.astype(jnp.float32) + selected).astype(jnp.bfloat16)
+    updated = selected.astype(jnp.bfloat16)
     return updated.reshape(step_count, row_count, model_width)
 
 

time: 132 us -> 140 us (1.061)
  local copies, waits for them, and re-layouts: 3.56 us -> 10.9 us
    reshape x1, local copies, waits for them, and re-layouts: 0.71 us -> 2.55 us  [shards(): flat_rows = arrived.reshape(experts * slots_per, model_width)]
    reshape x1, local copies, waits for them, and re-layouts: 0.71 us -> 2.55 us  [shards(): returned.reshape(experts * slots_per, model_width)]
    reshape x1, local copies, waits for them, and re-layouts: 0.73 us -> 2.55 us  [shards(): (flat_rows.astype(jnp.float32) + update).astype(jnp.bfloat16)]
    reshape x1, local copies, waits for them, and re-layouts: 0.73 us -> 2.55 us  [shards(): outgoing = outgoing.astype(jnp.bfloat16).reshape(packed)]
  transfers between devices with their start and end apart: 2 -> 2, of which waited for: 0 -> 0; matrix products, arithmetic and copies ran while one was open for 5% -> 7% of each run, Pallas kernels for 0% -> 0%
where the time goes in v11:
time: 140 us
  blocking collectives  104 us (74%)
  matrix products  22 us (16%)
  local copies, waits for them, and re-layouts  10.9 us (8%)
  other arithmetic  2.23 us (2%)
    all_to_all x1, blocking collectives, shards(): lax.all_to_all(outgoing, 'expert', split_axis=0, concat_axis=0, tiled=True)  56.5 us
    all_to_all x1, blocking collectives, shards(): lax.all_to_all(served, 'expert', split_axis=0, concat_axis=0, tiled=True)  47.8 us
    dot_general x1, matrix products, shards(): update = jnp.dot(hidden, down_full, preferred_element_type=jnp.float32)  17.9 us
  transfers between devices with their start and end apart: 2, of which 0 were waited for; matrix products, arithmetic and copies ran while one was open for 7% of the time, Pallas kernels for 0%

profile of v11, /device:TPU:32, one launch (start us, length us, event | category | flops | bytes accessed | tf_op | source)
XLA Modules:
  0.0 139.9 jit_solution(14582669248801692834)
XLA Ops:
  0.0 0.0 copy-start
  0.0 0.0 collective-permute-start
  0.0 0.5 collective-permute-start.1
  0.5 0.7 copy.9
  1.2 0.9 select_reduce_fusion.1
  2.2 0.8 fusion.22
  2.9 0.2 select_reduce_fusion
  3.1 0.2 convert_reduce_fusion
  3.4 0.1 add_bitcast_fusion
  3.4 0.0 copy-done
  3.4 2.3 %convolution_convert_fusion = bf16[768,1024]{1,0:T(8,128)(2,1)} fusion(bf16[384,1024]{1,0:T(8,128)(2,1)S(1)} %bitcast.12, s32[384]{0:T(512)S(1)} %add_bitcast_fusion), kind=kOutput, calls=%fused_computation.11 | convolution fusion | flops 605061120 | bytes 2360832 | tf_op jit(solution)/shard_map/rs,rd->sd/dot_general | solution.py:32
  5.8 2.5 %reshape.66 = bf16[128,48,128]{2,1,0:T(8,128)(2,1)S(1)} reshape(bf16[768,1024]{1,0:T(8,128)(2,1)} %convolution_convert_fusion) | data formatting | bytes 3145728 | tf_op jit(solution)/shard_map/reshape | solution.py:35
  8.3 56.5 %all_to_all.10 = bf16[128,48,128]{2,1,0:T(8,128)(2,1)} all-to-all(bf16[128,48,128]{2,1,0:T(8,128)(2,1)S(1)} %reshape.66), channel_id=1, replica_groups=mesh['dp'=2,'expert'=128] {'expert'}, dimensions={0} | all-to-all | bytes 3145728 | tf_op jit(solution)/shard_map/all_to_all | solution.py:36
  64.9 2.5 %reshape.67 = bf16[768,1024]{1,0:T(8,128)(2,1)S(1)} reshape(bf16[128,48,128]{2,1,0:T(8,128)(2,1)} %all_to_all.10) | data formatting | bytes 3145728 | tf_op jit(solution)/shard_map/reshape | solution.py:37
  67.4 0.0 collective-permute-done
  67.5 0.0 collective-permute-done.1
  67.5 17.9 %add_convert_fusion = bf16[768,1024]{1,0:T(8,128)(2,1)} fusion(bf16[768,1024]{1,0:T(8,128)(2,1)S(1)} %reshape.67, bf16[2048,1024]{1,0:T(8,128)(2,1)} %collective-permute-done.1, bf16[2048,1024]{1,0:T(8,128)(2,1)} %bitcast.15, bf16[1024,2048]{1,0:T(8,128)(2,1)} %collective-permute-done, bf16[1024,2048]{1,0:T(8,128)(2,1)} %bitcast.17), kind=kOutput, calls=%fused_computation.9 | convolution fusion | flops 12928679936 | bytes 19922944 | tf_op jit(solution)/shard_map/dot_general | solution.py:41
  85.4 2.5 %reshape.68 = bf16[128,48,128]{2,1,0:T(8,128)(2,1)S(1)} reshape(bf16[768,1024]{1,0:T(8,128)(2,1)} %add_convert_fusion) | data formatting | bytes 3145728 | tf_op jit(solution)/shard_map/reshape | solution.py:43
  87.9 47.8 %all_to_all.11 = bf16[128,48,128]{2,1,0:T(8,128)(2,1)} all-to-all(bf16[128,48,128]{2,1,0:T(8,128)(2,1)S(1)} %reshape.68), channel_id=1, replica_groups=mesh['dp'=2,'expert'=128] {'expert'}, dimensions={0} | all-to-all | bytes 3145728 | tf_op jit(solution)/shard_map/all_to_all | solution.py:44
  135.7 2.5 %reshape.69 = bf16[768,1024]{1,0:T(8,128)(2,1)S(1)} reshape(bf16[128,48,128]{2,1,0:T(8,128)(2,1)} %all_to_all.11) | data formatting | bytes 3145728 | tf_op jit(solution)/shard_map/reshape | solution.py:47
  138.2 1.7 %convolution_convert_fusion.1 = bf16[384,1024]{1,0:T(8,128)(2,1)} fusion(bf16[768,1024]{1,0:T(8,128)(2,1)S(1)} %reshape.69, s32[384]{0:T(512)S(1)} %add_bitcast_fusion), kind=kOutput, calls=%fused_computation.12 | convolution fusion | flops 604667904 | bytes 2360832 | tf_op jit(solution)/shard_map/dot_general | solution.py:45
  (3 shorter events, 0.0 us)
Async XLA Ops:
  0.0 3.4 %copy-start = (bf16[3,128,1024]{2,1,0:T(8,128)(2,1)S(1)}, bf16[3,128,1024]{2,1,0:T(8,128)(2,1)}, u32[]{:S(2)}) copy-start(bf16[3,128,1024]{2,1,0:T(8,128)(2,1)} %param.6) | copy-start | bytes 2359300
  0.0 67.4 %collective-permute-start = (bf16[1024,2048]{1,0:T(8,128)(2,1)}, bf16[1024,2048]{1,0:T(8,128)(2,1)}, u32[]{:S(2)}, u32[]{:S(2)}) collective-permute-start(bf16[1024,2048]{1,0:T(8,128)(2,1)} %bitcast.16), channel_id=1, source_target_pairs={{0,128},{128,0},{1,129},{129,1},{2,130},{130,2},{3,131},{131,3},{4... | collective-permute-start | bytes 12582920 | tf_op jit(solution)/shard_map/ppermute | solution.py:13
  0.0 67.4 %collective-permute-start.1 = (bf16[2048,1024]{1,0:T(8,128)(2,1)}, bf16[2048,1024]{1,0:T(8,128)(2,1)}, u32[]{:S(2)}, u32[]{:S(2)}) collective-permute-start(bf16[2048,1024]{1,0:T(8,128)(2,1)} %bitcast.14), channel_id=1, source_target_pairs={{0,128},{128,0},{1,129},{129,1},{2,130},{130,2},{3,131},{131,3},{4... | collective-permute-start | bytes 12582920 | tf_op jit(solution)/shard_map/ppermute | solution.py:14

commit v12 on v9

--- a/solution.py
+++ b/solution.py
@@ -29,7 +29,8 @@
     slot_labels = jnp.arange(experts * slots_per, dtype=jnp.int32)
     select = (slot_id[:, None] == slot_labels[None, :]).astype(jnp.bfloat16)
     rows = states.reshape(step_count * row_count, model_width)
-    outgoing = jnp.einsum("rs,rd->sd", select, rows, preferred_element_type=jnp.float32)
+    gather = (slot_labels[:, None] == slot_id[None, :]).astype(jnp.bfloat16)
+    outgoing = jnp.dot(gather, rows, preferred_element_type=jnp.float32)
     lanes = 128 if model_width % 128 == 0 else model_width
     packed = (experts, slots_per * model_width // lanes, lanes)
     outgoing = outgoing.astype(jnp.bfloat16).reshape(packed)

time: 132 us -> 132 us (level)
  no operation moved by 1% of the time
where the time goes in v12:
time: 132 us
  blocking collectives  104 us (79%)
  matrix products  21.5 us (16%)
  local copies, waits for them, and re-layouts  3.56 us (3%)
  other arithmetic  2.23 us (2%)
    all_to_all x1, blocking collectives, shards(): lax.all_to_all(outgoing, 'expert', split_axis=0, concat_axis=0, tiled=True)  56.3 us
    all_to_all x1, blocking collectives, shards(): lax.all_to_all(served, 'expert', split_axis=0, concat_axis=0, tiled=True)  47.7 us
    dot_general x1, matrix products, shards(): update = jnp.dot(hidden, down_full, preferred_element_type=jnp.float32)  16.6 us
    dot_general x1, matrix products, shards(): jnp.dot(select, returned.reshape(experts * slots_per, model_width), prefe...  2.84 us
  transfers between devices with their start and end apart: 2, of which 0 were waited for; matrix products, arithmetic and copies ran while one was open for 5% of the time, Pallas kernels for 0%

profile of v12, /device:TPU:32, one launch (start us, length us, event | category | flops | bytes accessed | tf_op | source)
XLA Modules:
  0.0 131.9 jit_solution(11172535464835596049)
XLA Ops:
  0.0 0.0 collective-permute-start
  0.0 0.5 collective-permute-start.1
  0.5 0.7 copy.9
  1.2 0.9 select_reduce_fusion.1
  2.2 0.8 fusion.18
  2.9 0.2 select_reduce_fusion
  3.1 0.2 convert_reduce_fusion
  3.4 0.1 add_bitcast_fusion
  3.4 2.1 %convolution_convert_fusion = bf16[768,1024]{1,0:T(8,128)(2,1)S(1)} fusion(bf16[384,1024]{1,0:T(8,128)(2,1)} %bitcast.17, s32[384]{0:T(512)S(1)} %add_bitcast_fusion), kind=kOutput, calls=%fused_computation.10 | convolution fusion | flops 605061120 | bytes 2360832 | tf_op jit(solution)/shard_map/dot_general | solution.py:33
  5.6 0.7 reshape.83
  6.3 56.3 %all_to_all.10 = bf16[128,48,128]{2,1,0:T(8,128)(2,1)S(1)} all-to-all(bf16[128,48,128]{2,1,0:T(8,128)(2,1)S(1)} %reshape.83), channel_id=1, replica_groups=mesh['dp'=2,'expert'=128] {'expert'}, dimensions={0} | all-to-all | bytes 3145728 | tf_op jit(solution)/shard_map/all_to_all | solution.py:37
  62.6 0.7 reshape.84
  63.4 0.0 collective-permute-done
  63.4 0.0 collective-permute-done.1
  63.4 16.6 %fusion.10 = bf16[768,1024]{1,0:T(8,128)(2,1)S(1)} fusion(bf16[2048,1024]{1,0:T(8,128)(2,1)} %collective-permute-done.1, bf16[2048,1024]{1,0:T(8,128)(2,1)} %bitcast.14, bf16[768,1024]{1,0:T(8,128)(2,1)S(1)} %reshape.84, bf16[1024,2048]{1,0:T(8,128)(2,1)} %collective-permute-done, bf16[1024,2048]{1,0:T(8,128)(2,1)} %bitcast.16), kind=kOutput, calls=%fused_computation.9 | convolution fusion | flops 12925534208 | bytes 19922944 | tf_op jit(solution)/shard_map/dot_general | solution.py:42
  80.0 0.7 reshape.85
  80.7 47.7 %all_to_all.11 = bf16[128,48,128]{2,1,0:T(8,128)(2,1)S(1)} all-to-all(bf16[128,48,128]{2,1,0:T(8,128)(2,1)S(1)} %reshape.85), channel_id=1, replica_groups=mesh['dp'=2,'expert'=128] {'expert'}, dimensions={0} | all-to-all | bytes 3145728 | tf_op jit(solution)/shard_map/all_to_all | solution.py:44
  128.4 0.7 reshape.86
  129.1 2.8 %add_convert_fusion = bf16[384,1024]{1,0:T(8,128)(2,1)} fusion(bf16[384,1024]{1,0:T(8,128)(2,1)} %bitcast.18, bf16[768,1024]{1,0:T(8,128)(2,1)S(1)} %reshape.86, s32[384]{0:T(512)S(1)} %add_bitcast_fusion), kind=kOutput, calls=%fused_computation.11 | convolution fusion | flops 605454336 | bytes 3147264 | tf_op jit(solution)/shard_map/dot_general | solution.py:45
  (3 shorter events, 0.0 us)
Async XLA Ops:
  0.0 63.4 %collective-permute-start = (bf16[1024,2048]{1,0:T(8,128)(2,1)}, bf16[1024,2048]{1,0:T(8,128)(2,1)}, u32[]{:S(2)}, u32[]{:S(2)}) collective-permute-start(bf16[1024,2048]{1,0:T(8,128)(2,1)} %bitcast.15), channel_id=1, source_target_pairs={{0,128},{128,0},{1,129},{129,1},{2,130},{130,2},{3,131},{131,3},{4... | collective-permute-start | bytes 12582920 | tf_op jit(solution)/shard_map/ppermute | solution.py:13
  0.0 63.4 %collective-permute-start.1 = (bf16[2048,1024]{1,0:T(8,128)(2,1)}, bf16[2048,1024]{1,0:T(8,128)(2,1)}, u32[]{:S(2)}, u32[]{:S(2)}) collective-permute-start(bf16[2048,1024]{1,0:T(8,128)(2,1)} %bitcast.13), channel_id=1, source_target_pairs={{0,128},{128,0},{1,129},{129,1},{2,130},{130,2},{3,131},{131,3},{4... | collective-permute-start | bytes 12582920 | tf_op jit(solution)/shard_map/ppermute | solution.py:14

commit v13 on v9

--- a/solution.py
+++ b/solution.py
@@ -12,8 +12,6 @@
     pair = [(0, 1), (1, 0)]
     other_up = lax.ppermute(up_weight[0], "dp", pair)
     other_down = lax.ppermute(down_weight[0], "dp", pair)
-    up_full = jnp.concatenate([up_weight[0], other_up], axis=1)
-    down_full = jnp.concatenate([down_weight[0], other_down], axis=0)
     slots_per = step_count * capacity
     steps = jnp.arange(step_count, dtype=jnp.int32)
     placed_hot = placement[:, :, None] == labels[None, None, :]
@@ -35,10 +33,13 @@
     outgoing = outgoing.astype(jnp.bfloat16).reshape(packed)
     arrived = lax.all_to_all(outgoing, "expert", split_axis=0, concat_axis=0, tiled=True)
     flat_rows = arrived.reshape(experts * slots_per, model_width)
-    hidden = jnp.maximum(
-        jnp.dot(flat_rows, up_full, preferred_element_type=jnp.float32), 0.0
-    ).astype(jnp.bfloat16)
-    update = jnp.dot(hidden, down_full, preferred_element_type=jnp.float32)
+    def half_ffn(up_half, down_half):
+        hidden = jnp.maximum(
+            jnp.dot(flat_rows, up_half, preferred_element_type=jnp.float32), 0.0
+        ).astype(jnp.bfloat16)
+        return jnp.dot(hidden, down_half, preferred_element_type=jnp.float32)
+
+    update = half_ffn(up_weight[0], down_weight[0]) + half_ffn(other_up, other_down)
     served = update.astype(jnp.bfloat16).reshape(packed)
     returned = lax.all_to_all(served, "expert", split_axis=0, concat_axis=0, tiled=True)
     selected = jnp.dot(

time: 132 us -> 143 us (1.083)
  blocking collectives: 104 us -> 47.9 us
  waiting for transfers between devices: 0.01 us -> 40.5 us
  starting transfers between devices: 0.51 us -> 15.6 us
  matrix products: 21.7 us -> 29.2 us
  local copies, waits for them, and re-layouts: 3.56 us -> 6.76 us
    all_to_all x1 -> x0, blocking collectives: 56.3 us -> none  [shards(): lax.all_to_all(outgoing, 'expert', split_axis=0, concat_axis=0, tiled=True)]
    all_to_all x0 -> x1, waiting for transfers between devices: none -> 40.5 us  [shards(): lax.all_to_all(outgoing, 'expert', split_axis=0, concat_axis=0, tiled=True)]
    all_to_all x0 -> x1, starting transfers between devices: none -> 15 us  [shards(): lax.all_to_all(outgoing, 'expert', split_axis=0, concat_axis=0, tiled=True)]
    dot_general x1 -> x2, matrix products: 16.6 us -> 24.1 us  [half_ffn(): return jnp.dot(hidden, down_half, preferred_element_type=jnp.float32)]
    reshape x1, local copies, waits for them, and re-layouts: 0.73 us -> 2.55 us  [shards(): served = update.astype(jnp.bfloat16).reshape(packed)]
  transfers between devices with their start and end apart: 2 -> 3, of which waited for: 0 -> 1; matrix products, arithmetic and copies ran while one was open for 5% -> 9% of each run, Pallas kernels for 0% -> 0%
where the time goes in v13:
time: 143 us; the launch traced here: 142 us
  blocking collectives  47.9 us (33%)
  waiting for transfers between devices  40.5 us (28%)
  matrix products  29.2 us (20%)
  starting transfers between devices  15.6 us (11%)
  local copies, waits for them, and re-layouts  6.76 us (5%)
  other arithmetic  2.24 us (2%)
    all_to_all x1, blocking collectives, shards(): lax.all_to_all(served, 'expert', split_axis=0, concat_axis=0, tiled=True)  47.9 us
    all_to_all x1, waiting for transfers between devices, shards(): lax.all_to_all(outgoing, 'expert', split_axis=0, concat_axis=0, tiled=True)  40.5 us
    dot_general x2, matrix products, half_ffn(): return jnp.dot(hidden, down_half, preferred_element_type=jnp.float32)  24.1 us
    all_to_all x1, starting transfers between devices, shards(): lax.all_to_all(outgoing, 'expert', split_axis=0, concat_axis=0, tiled=True)  15 us
  transfers between devices with their start and end apart: 3, of which 1 were waited for; matrix products, arithmetic and copies ran while one was open for 9% of the time, Pallas kernels for 0%

profile of v13, /device:TPU:32, one launch (start us, length us, event | category | flops | bytes accessed | tf_op | source)
XLA Modules:
  0.0 142.3 jit_solution(3008009249191833997)
XLA Ops:
  0.0 0.7 copy.9
  0.7 0.9 select_reduce_fusion.1
  1.6 0.8 fusion.4
  2.4 0.2 select_reduce_fusion
  2.6 0.2 convert_reduce_fusion
  2.9 0.1 add_bitcast_fusion
  2.9 2.2 %convolution_convert_fusion = bf16[768,1024]{1,0:T(8,128)(2,1)S(1)} fusion(bf16[384,1024]{1,0:T(8,128)(2,1)} %bitcast.23, s32[384]{0:T(512)S(1)} %add_bitcast_fusion), kind=kOutput, calls=%fused_computation.3 | convolution fusion | flops 605061120 | bytes 2360832 | tf_op jit(solution)/shard_map/rs,rd->sd/dot_general | solution.py:30
  5.2 2.1 %reshape.66 = bf16[128,48,128]{2,1,0:T(8,128)(2,1)} reshape(bf16[768,1024]{1,0:T(8,128)(2,1)S(1)} %convolution_convert_fusion) | data formatting | bytes 3145728 | tf_op jit(solution)/shard_map/reshape | solution.py:33
  7.3 15.0 %all-to-all-start = ((bf16[128,48,128]{2,1,0:T(8,128)(2,1)}), bf16[128,48,128]{2,1,0:T(8,128)(2,1)S(1)}, u32[]{:S(2)}, u32[]{:S(2)}) async-start(bf16[128,48,128]{2,1,0:T(8,128)(2,1)} %reshape.66), calls=%async_computation | async-start | bytes 3145728 | tf_op jit(solution)/shard_map/all_to_all | solution.py:34
  22.3 0.1 collective-permute-start.1
  22.4 0.5 collective-permute-start
  22.9 40.5 %all-to-all-done = bf16[128,48,128]{2,1,0:T(8,128)(2,1)S(1)} async-done(((bf16[128,48,128]{2,1,0:T(8,128)(2,1)}), bf16[128,48,128]{2,1,0:T(8,128)(2,1)S(1)}, u32[]{:S(2)}, u32[]{:S(2)}) %all-to-all-start) | async-done | bytes 1572896 | tf_op jit(solution)/shard_map/all_to_all | solution.py:34
  63.4 0.7 reshape.67
  64.1 11.9 %fusion = f32[768,1024]{1,0:T(8,128)} fusion(bf16[768,1024]{1,0:T(8,128)(2,1)S(1)} %reshape.67, bf16[1,2048,1024]{2,1,0:T(8,128)(2,1)} %param.11, bf16[1,1024,2048]{2,1,0:T(8,128)(2,1)} %param.10), kind=kOutput, calls=%fused_computation.6 | convolution fusion | flops 6445596672 | bytes 13107200 | tf_op jit(solution)/shard_map/dot_general | solution.py:40
  76.0 0.0 collective-permute-done.1
  76.0 0.0 collective-permute-done
  76.0 12.2 %add_convert_fusion = bf16[768,1024]{1,0:T(8,128)(2,1)} fusion(f32[768,1024]{1,0:T(8,128)} %fusion, bf16[2048,1024]{1,0:T(8,128)(2,1)} %collective-permute-done.1, bf16[768,1024]{1,0:T(8,128)(2,1)S(1)} %reshape.67, bf16[1024,2048]{1,0:T(8,128)(2,1)} %collective-permute-done), kind=kOutput, calls=%fused_computation.2 | convolution fusion | flops 6447169536 | bytes 14680064 | tf_op jit(solution)/shard_map/dot_general | solution.py:40
  88.2 2.5 %reshape.68 = bf16[128,48,128]{2,1,0:T(8,128)(2,1)S(1)} reshape(bf16[768,1024]{1,0:T(8,128)(2,1)} %add_convert_fusion) | data formatting | bytes 3145728 | tf_op jit(solution)/shard_map/reshape | solution.py:43
  90.8 47.9 %all_to_all.10 = bf16[128,48,128]{2,1,0:T(8,128)(2,1)S(1)} all-to-all(bf16[128,48,128]{2,1,0:T(8,128)(2,1)S(1)} %reshape.68), channel_id=1, replica_groups=mesh['dp'=2,'expert'=128] {'expert'}, dimensions={0} | all-to-all | bytes 3145728 | tf_op jit(solution)/shard_map/all_to_all | solution.py:44
  138.7 0.7 reshape.69
  139.4 2.9 %add_convert_fusion.1 = bf16[384,1024]{1,0:T(8,128)(2,1)} fusion(bf16[384,1024]{1,0:T(8,128)(2,1)} %bitcast.24, bf16[768,1024]{1,0:T(8,128)(2,1)S(1)} %reshape.69, s32[384]{0:T(512)S(1)} %add_bitcast_fusion), kind=kOutput, calls=%fused_computation.4 | convolution fusion | flops 605454336 | bytes 3147264 | tf_op jit(solution)/shard_map/dot_general | solution.py:45
  (3 shorter events, 0.0 us)
Async XLA Ops:
  7.3 56.1 %all-to-all-start = ((bf16[128,48,128]{2,1,0:T(8,128)(2,1)}), bf16[128,48,128]{2,1,0:T(8,128)(2,1)S(1)}, u32[]{:S(2)}, u32[]{:S(2)}) async-start(bf16[128,48,128]{2,1,0:T(8,128)(2,1)} %reshape.66), calls=%async_computation | async-start | bytes 3145728 | tf_op jit(solution)/shard_map/all_to_all | solution.py:34
  22.3 53.7 %collective-permute-start.1 = (bf16[2048,1024]{1,0:T(8,128)(2,1)}, bf16[2048,1024]{1,0:T(8,128)(2,1)}, u32[]{:S(2)}, u32[]{:S(2)}) collective-permute-start(bf16[2048,1024]{1,0:T(8,128)(2,1)} %bitcast.21), channel_id=1, source_target_pairs={{0,128},{128,0},{1,129},{129,1},{2,130},{130,2},{3,131},{131,3},{4... | collective-permute-start | bytes 12582920 | tf_op jit(solution)/shard_map/ppermute | solution.py:14
  22.4 53.6 %collective-permute-start = (bf16[1024,2048]{1,0:T(8,128)(2,1)}, bf16[1024,2048]{1,0:T(8,128)(2,1)}, u32[]{:S(2)}, u32[]{:S(2)}) collective-permute-start(bf16[1024,2048]{1,0:T(8,128)(2,1)} %bitcast.22), channel_id=1, source_target_pairs={{0,128},{128,0},{1,129},{129,1},{2,130},{130,2},{3,131},{131,3},{4... | collective-permute-start | bytes 12582920 | tf_op jit(solution)/shard_map/ppermute | solution.py:13

commit v14 on v9

--- a/solution.py
+++ b/solution.py
@@ -36,7 +36,12 @@
     arrived = lax.all_to_all(outgoing, "expert", split_axis=0, concat_axis=0, tiled=True)
     flat_rows = arrived.reshape(experts * slots_per, model_width)
     hidden = jnp.maximum(
-        jnp.dot(flat_rows, up_full, preferred_element_type=jnp.float32), 0.0
+        jnp.einsum(
+            "dcl,clh->dh",
+            arrived.reshape(experts * slots_per, model_width // lanes, lanes),
+            up_full.reshape(model_width // lanes, lanes, up_full.shape[1]),
+            preferred_element_type=jnp.float32,
+        ), 0.0
     ).astype(jnp.bfloat16)
     update = jnp.dot(hidden, down_full, preferred_element_type=jnp.float32)
     served = update.astype(jnp.bfloat16).reshape(packed)

time: 132 us -> 132 us (level)
  transfers between devices with their start and end apart: 2 -> 2, of which waited for: 0 -> 0; matrix products, arithmetic and copies ran while one was open for 5% -> 4% of each run, Pallas kernels for 0% -> 0%
where the time goes in v14:
time: 132 us; the launch traced here: 131 us
  blocking collectives  104 us (79%)
  matrix products  21.7 us (16%)
  local copies, waits for them, and re-layouts  2.85 us (2%)
  other arithmetic  2.23 us (2%)
    all_to_all x1, blocking collectives, shards(): lax.all_to_all(outgoing, 'expert', split_axis=0, concat_axis=0, tiled=True)  56.3 us
    all_to_all x1, blocking collectives, shards(): lax.all_to_all(served, 'expert', split_axis=0, concat_axis=0, tiled=True)  47.7 us
    dot_general x1, matrix products, shards(): update = jnp.dot(hidden, down_full, preferred_element_type=jnp.float32)  16.6 us
    dot_general x1, matrix products, shards(): jnp.dot(select, returned.reshape(experts * slots_per, model_width), prefe...  2.86 us
  transfers between devices with their start and end apart: 2, of which 0 were waited for; matrix products, arithmetic and copies ran while one was open for 4% of the time, Pallas kernels for 0%

profile of v14, /device:TPU:32, one launch (start us, length us, event | category | flops | bytes accessed | tf_op | source)
XLA Modules:
  0.0 131.4 jit_solution(8074064333734683605)
XLA Ops:
  0.0 0.0 collective-permute-start.1
  0.0 0.5 collective-permute-start
  0.5 0.7 copy.13
  1.2 0.9 select_reduce_fusion.1
  2.2 0.8 fusion.23
  2.9 0.2 select_reduce_fusion
  3.1 0.2 convert_reduce_fusion
  3.4 0.1 add_bitcast_fusion
  3.4 2.2 %convolution_convert_fusion = bf16[768,1024]{1,0:T(8,128)(2,1)S(1)} fusion(bf16[384,1024]{1,0:T(8,128)(2,1)} %bitcast.28, s32[384]{0:T(512)S(1)} %add_bitcast_fusion), kind=kOutput, calls=%fused_computation.11 | convolution fusion | flops 605061120 | bytes 2360832 | tf_op jit(solution)/shard_map/rs,rd->sd/dot_general | solution.py:32
  5.7 0.7 reshape.70
  6.4 56.3 %all_to_all.10 = bf16[128,48,128]{2,1,0:T(8,128)(2,1)S(1)} all-to-all(bf16[128,48,128]{2,1,0:T(8,128)(2,1)S(1)} %reshape.70), channel_id=1, replica_groups=mesh['dp'=2,'expert'=128] {'expert'}, dimensions={0} | all-to-all | bytes 3145728 | tf_op jit(solution)/shard_map/all_to_all | solution.py:36
  62.8 0.0 collective-permute-done.1
  62.8 0.0 collective-permute-done
  62.8 16.6 %fusion.13 = bf16[768,1024]{1,0:T(8,128)(2,1)S(1)} fusion(bf16[2048,1024]{1,0:T(8,128)(2,1)} %collective-permute-done.1, bf16[2048,1024]{1,0:T(8,128)(2,1)} %bitcast.25, bf16[8,128,2048]{2,1,0:T(8,128)(2,1)} %bitcast.5, bf16[8,128,2048]{2,1,0:T(8,128)(2,1)} %bitcast.27, bf16[768,8,128]{2,1,0:T(8,128)(2,1)S(1)} %bitcast.22), kind=kOutput, calls=%fused_computation.10 | convolution fusion | flops 12925534208 | bytes 19922944 | tf_op jit(solution)/shard_map/dot_general | solution.py:46
  79.4 0.7 reshape.72
  80.1 47.7 %all_to_all.11 = bf16[128,48,128]{2,1,0:T(8,128)(2,1)S(1)} all-to-all(bf16[128,48,128]{2,1,0:T(8,128)(2,1)S(1)} %reshape.72), channel_id=1, replica_groups=mesh['dp'=2,'expert'=128] {'expert'}, dimensions={0} | all-to-all | bytes 3145728 | tf_op jit(solution)/shard_map/all_to_all | solution.py:48
  127.8 0.7 reshape.73
  128.5 2.9 %add_convert_fusion = bf16[384,1024]{1,0:T(8,128)(2,1)} fusion(bf16[384,1024]{1,0:T(8,128)(2,1)} %bitcast.29, bf16[768,1024]{1,0:T(8,128)(2,1)S(1)} %reshape.73, s32[384]{0:T(512)S(1)} %add_bitcast_fusion), kind=kOutput, calls=%fused_computation.13 | convolution fusion | flops 605454336 | bytes 3147264 | tf_op jit(solution)/shard_map/dot_general | solution.py:49
  (3 shorter events, 0.0 us)
Async XLA Ops:
  0.0 62.8 %collective-permute-start.1 = (bf16[2048,1024]{1,0:T(8,128)(2,1)}, bf16[2048,1024]{1,0:T(8,128)(2,1)}, u32[]{:S(2)}, u32[]{:S(2)}) collective-permute-start(bf16[2048,1024]{1,0:T(8,128)(2,1)} %bitcast.24), channel_id=1, source_target_pairs={{0,128},{128,0},{1,129},{129,1},{2,130},{130,2},{3,131},{131,3},{4... | collective-permute-start | bytes 12582920 | tf_op jit(solution)/shard_map/ppermute | solution.py:14
  0.0 62.8 %collective-permute-start = (bf16[1024,2048]{1,0:T(8,128)(2,1)}, bf16[1024,2048]{1,0:T(8,128)(2,1)}, u32[]{:S(2)}, u32[]{:S(2)}) collective-permute-start(bf16[1024,2048]{1,0:T(8,128)(2,1)} %bitcast.26), channel_id=1, source_target_pairs={{0,128},{128,0},{1,129},{129,1},{2,130},{130,2},{3,131},{131,3},{4... | collective-permute-start | bytes 12582920 | tf_op jit(solution)/shard_map/ppermute | solution.py:13

commit v15 on v14

--- a/solution.py
+++ b/solution.py
@@ -46,11 +46,12 @@
     update = jnp.dot(hidden, down_full, preferred_element_type=jnp.float32)
     served = update.astype(jnp.bfloat16).reshape(packed)
     returned = lax.all_to_all(served, "expert", split_axis=0, concat_axis=0, tiled=True)
-    selected = jnp.dot(
+    selected = jnp.einsum(
+        "rs,scl->rcl",
         select,
-        returned.reshape(experts * slots_per, model_width),
+        returned.reshape(experts * slots_per, model_width // lanes, lanes),
         preferred_element_type=jnp.float32,
-    )
+    ).reshape(step_count * row_count, model_width)
     updated = (rows.astype(jnp.float32) + selected).astype(jnp.bfloat16)
     return updated.reshape(step_count, row_count, model_width)
 

time: 132 us -> 131 us (level)
  transfers between devices with their start and end apart: 2 -> 2, of which waited for: 0 -> 0; matrix products, arithmetic and copies ran while one was open for 4% -> 5% of each run, Pallas kernels for 0% -> 0%
where the time goes in v15:
time: 131 us
  blocking collectives  104 us (79%)
  matrix products  21.7 us (17%)
  other arithmetic  2.23 us (2%)
  local copies, waits for them, and re-layouts  2.14 us (2%)
    all_to_all x1, blocking collectives, shards(): lax.all_to_all(outgoing, 'expert', split_axis=0, concat_axis=0, tiled=True)  56.3 us
    all_to_all x1, blocking collectives, shards(): lax.all_to_all(served, 'expert', split_axis=0, concat_axis=0, tiled=True)  47.7 us
    dot_general x1, matrix products, shards(): update = jnp.dot(hidden, down_full, preferred_element_type=jnp.float32)  16.6 us
    dot_general x1, matrix products, shards(): jnp.einsum('rs,scl->rcl', select, returned.reshape(experts * slots_per, m...  2.84 us
  transfers between devices with their start and end apart: 2, of which 0 were waited for; matrix products, arithmetic and copies ran while one was open for 5% of the time, Pallas kernels for 0%

profile of v15, /device:TPU:32, one launch (start us, length us, event | category | flops | bytes accessed | tf_op | source)
XLA Modules:
  0.0 130.6 jit_solution(2703911824297276657)
XLA Ops:
  0.0 0.0 collective-permute-start.1
  0.0 0.5 collective-permute-start
  0.5 0.7 copy.20
  1.2 0.9 select_reduce_fusion.1
  2.2 0.8 fusion.28
  2.9 0.2 select_reduce_fusion
  3.1 0.2 convert_reduce_fusion
  3.4 0.1 add_bitcast_fusion
  3.4 2.2 %convolution_convert_fusion = bf16[768,1024]{1,0:T(8,128)(2,1)S(1)} fusion(bf16[384,1024]{1,0:T(8,128)(2,1)} %bitcast.39, s32[384]{0:T(512)S(1)} %add_bitcast_fusion), kind=kOutput, calls=%fused_computation.11 | convolution fusion | flops 605061120 | bytes 2360832 | tf_op jit(solution)/shard_map/rs,rd->sd/dot_general | solution.py:32
  5.7 0.7 reshape.72
  6.4 56.3 %all_to_all.10 = bf16[128,48,128]{2,1,0:T(8,128)(2,1)S(1)} all-to-all(bf16[128,48,128]{2,1,0:T(8,128)(2,1)S(1)} %reshape.72), channel_id=1, replica_groups=mesh['dp'=2,'expert'=128] {'expert'}, dimensions={0} | all-to-all | bytes 3145728 | tf_op jit(solution)/shard_map/all_to_all | solution.py:36
  62.8 0.0 collective-permute-done.1
  62.8 0.0 collective-permute-done
  62.8 16.6 %fusion.13 = bf16[768,1024]{1,0:T(8,128)(2,1)S(1)} fusion(bf16[2048,1024]{1,0:T(8,128)(2,1)} %collective-permute-done.1, bf16[2048,1024]{1,0:T(8,128)(2,1)} %bitcast.36, bf16[8,128,2048]{2,1,0:T(8,128)(2,1)} %bitcast.5, bf16[8,128,2048]{2,1,0:T(8,128)(2,1)} %bitcast.38, bf16[768,8,128]{2,1,0:T(8,128)(2,1)S(1)} %bitcast.32), kind=kOutput, calls=%fused_computation.10 | convolution fusion | flops 12925534208 | bytes 19922944 | tf_op jit(solution)/shard_map/dot_general | solution.py:46
  79.4 0.7 reshape.74
  80.1 47.7 %all_to_all.11 = bf16[128,48,128]{2,1,0:T(8,128)(2,1)S(1)} all-to-all(bf16[128,48,128]{2,1,0:T(8,128)(2,1)S(1)} %reshape.74), channel_id=1, replica_groups=mesh['dp'=2,'expert'=128] {'expert'}, dimensions={0} | all-to-all | bytes 3145728 | tf_op jit(solution)/shard_map/all_to_all | solution.py:48
  127.8 2.8 %add_convert_fusion = bf16[384,1024]{1,0:T(8,128)(2,1)} fusion(bf16[384,1024]{1,0:T(8,128)(2,1)} %bitcast.40, bf16[96,8,8,128]{3,2,1,0:T(8,128)(2,1)S(1)} %bitcast.33, s32[384]{0:T(512)S(1)} %add_bitcast_fusion), kind=kOutput, calls=%fused_computation.16 | convolution fusion | flops 605454336 | bytes 3147264 | tf_op jit(solution)/shard_map/rs,scl->rcl/dot_general | solution.py:49
  (3 shorter events, 0.0 us)
Async XLA Ops:
  0.0 62.8 %collective-permute-start.1 = (bf16[2048,1024]{1,0:T(8,128)(2,1)}, bf16[2048,1024]{1,0:T(8,128)(2,1)}, u32[]{:S(2)}, u32[]{:S(2)}) collective-permute-start(bf16[2048,1024]{1,0:T(8,128)(2,1)} %bitcast.35), channel_id=1, source_target_pairs={{0,128},{128,0},{1,129},{129,1},{2,130},{130,2},{3,131},{131,3},{4... | collective-permute-start | bytes 12582920 | tf_op jit(solution)/shard_map/ppermute | solution.py:14
  0.0 62.8 %collective-permute-start = (bf16[1024,2048]{1,0:T(8,128)(2,1)}, bf16[1024,2048]{1,0:T(8,128)(2,1)}, u32[]{:S(2)}, u32[]{:S(2)}) collective-permute-start(bf16[1024,2048]{1,0:T(8,128)(2,1)} %bitcast.37), channel_id=1, source_target_pairs={{0,128},{128,0},{1,129},{129,1},{2,130},{130,2},{3,131},{131,3},{4... | collective-permute-start | bytes 12582920 | tf_op jit(solution)/shard_map/ppermute | solution.py:13
